TPU v7x, 256 devices: a whole 4x4x8 slice. The times are simulated.
256 devices in a mesh: pts: 128 (over y, z, x), rep: 2 (over core).
Axes of the slice: x: 4, y: 4, z: 8, core: 2. Of those that a mesh axis runs over, the one named last changes fastest.
Arguments:
- src_points: bfloat16 [393216, 256], P('pts'), may hold values from -7 to 7
- tgt_points: bfloat16 [393216, 256], P('pts'), may hold values from -7 to 7
- pair_source: int32 [24576], P(('pts', 'rep')), may hold values from -1 to 3071, as said below
- pair_target: int32 [24576], P(('pts', 'rep')), may hold values from -1 to 3071, as said below
- pair_count: int32 [256], P(('pts', 'rep')), may hold values from 12 to 96, as said below
Outputs:
- source_dual: float32 [393216], P('pts')
- target_dual: float32 [393216], P('pts')
- target_grad: float32 [393216, 256], P('pts')
Inputs may be any that keep to these rules, and one draw needn't show every extreme that they name: `pair_source`: for the device at index d of pts+rep (pts index p = d // 2, rep index r = d % 2), the first pair_count[d] of its 96 slots name source blocks p * 24 to (p + 1) * 24 - 1; its other slots hold -1. `pair_target`: A listed target block t has owner t // 24; one device's listed slots name different owners, and only blocks whose index t % 24 lies in r * 12 to (r + 1) * 12 - 1; unlisted slots hold -1. No pair of blocks is listed twice; every source block and every target block is listed somewhere; some owner is named by every device. `pair_count`: some device lists 96 pairs.
All inputs are finite; a program needn't handle non-finite values.
Results may differ from a plain program's by a relative error of at most 0.0016.
Values may be sent and summed in bfloat16 or wider, within the bound.
No kernel may reach another device: no remote copies, remote signals or barrier semaphores. Data moves between devices by JAX's collectives and lax.ppermute only.
A program may use at most 192 MiB of HBM per device.

v0:
```python
import jax
import jax.numpy as jnp
from jax import lax
from jax.sharding import PartitionSpec as P

BLOCK = 128
ITERS = 3


EPSILON = 0.05
NEG_BIG = -1e30


def joined(part, axis, combine):
    gathered = jax.tree.map(lambda a: lax.all_gather(a, axis), part)

    def take(source):
        return jax.tree.map(lambda a: lax.dynamic_index_in_dim(a, source, 0, False), gathered)

    return lax.fori_loop(
        1, lax.axis_size(axis), lambda source, state: combine(state, take(source)), take(0)
    )


def squares(blocks_in):
    return jnp.sum(jnp.square(blocks_in.astype(jnp.float32)), axis=-1)


def pair_costs(source_rows, target_rows, source_sq, target_sq):
    inner_dot = jnp.einsum(
        "gid,gjd->gij", source_rows, target_rows, preferred_element_type=jnp.float32
    )
    return (source_sq[:, :, None] + target_sq[:, None, :] - 2.0 * inner_dot) / source_rows.shape[2]


def pair_sweep(arranged, pair_total, visit, initial):
    source_slots, source_sq_slots, target_slots, target_sq_slots = arranged

    def advance(group_no, carry):
        first_row = group_no * 8
        in_use = first_row + jnp.arange(8) < pair_total
        source_rows = lax.dynamic_slice_in_dim(source_slots, first_row, 8)
        target_rows = lax.dynamic_slice_in_dim(target_slots, first_row, 8)
        source_sq = lax.dynamic_slice_in_dim(source_sq_slots, first_row, 8)
        target_sq = lax.dynamic_slice_in_dim(target_sq_slots, first_row, 8)
        cost_grid = pair_costs(source_rows, target_rows, source_sq, target_sq)
        return visit(carry, cost_grid, source_rows, in_use, first_row)

    return lax.fori_loop(0, (pair_total + 7) // 8, advance, initial)


def store_stats(carry, peaks, masses, in_use, first_row):
    peaks = jnp.where(in_use[:, None], peaks, NEG_BIG)
    masses = jnp.where(in_use[:, None], masses, 0.0)
    return (
        lax.dynamic_update_slice_in_dim(carry[0], peaks, first_row, 0),
        lax.dynamic_update_slice_in_dim(carry[1], masses, first_row, 0),
    )


def row_visit(target_dual_slots):

    def visit(carry, cost_grid, source_rows, in_use, first_row):
        duals_here = lax.dynamic_slice_in_dim(target_dual_slots, first_row, 8)
        scores = (duals_here[:, None, :] - cost_grid) / EPSILON
        peaks = jnp.max(scores, axis=2)
        masses = jnp.sum(jnp.exp(scores - peaks[:, :, None]), axis=2)
        return store_stats(carry, peaks, masses, in_use, first_row)

    return visit


def column_visit(source_dual_slots):

    def visit(carry, cost_grid, source_rows, in_use, first_row):
        duals_here = lax.dynamic_slice_in_dim(source_dual_slots, first_row, 8)
        scores = (duals_here[:, :, None] - cost_grid) / EPSILON
        peaks = jnp.max(scores, axis=1)
        masses = jnp.sum(jnp.exp(scores - peaks[:, None, :]), axis=1)
        return store_stats(carry, peaks, masses, in_use, first_row)

    return visit


def gradient_visit(source_dual_slots, target_dual_slots):

    def visit(carry, cost_grid, source_rows, in_use, first_row):
        partials, masses = carry
        source_here = lax.dynamic_slice_in_dim(source_dual_slots, first_row, 8)
        target_here = lax.dynamic_slice_in_dim(target_dual_slots, first_row, 8)
        plan = jnp.exp((source_here[:, :, None] + target_here[:, None, :] - cost_grid) / EPSILON)
        plan = jnp.where(in_use[:, None, None], plan, 0.0)
        partial_value = jnp.einsum(
            "gij,gid->gjd",
            plan.astype(jnp.bfloat16),
            source_rows,
            preferred_element_type=jnp.float32,
        )
        partials = lax.dynamic_update_slice_in_dim(partials, partial_value, first_row, 0)
        masses = lax.dynamic_update_slice_in_dim(masses, jnp.sum(plan, axis=1), first_row, 0)
        return (partials, masses)

    return visit


def fresh_stats(length, block_len):
    return (
        jnp.full((length, block_len), NEG_BIG, jnp.float32),
        jnp.zeros((length, block_len), jnp.float32),
    )


def combine_by(peaks, masses, block_key, key_count):
    member = (block_key[:, None] == jnp.arange(key_count)[None, :])[:, :, None]
    maxima = jnp.max(jnp.where(member, peaks[:, None, :], NEG_BIG), axis=0)
    shifts = jnp.where(member, peaks[:, None, :] - maxima[None, :, :], NEG_BIG)
    totals = jnp.sum(jnp.where(member, masses[:, None, :] * jnp.exp(shifts), 0.0), axis=0)
    return (maxima, totals)


def merge_logsum(former, latter):
    maxima = jnp.maximum(former[0], latter[0])
    return (
        maxima,
        former[1] * jnp.exp(former[0] - maxima) + latter[1] * jnp.exp(latter[0] - maxima),
    )


def settle_sources(peaks, masses, block_key, key_count):
    maxima, totals = combine_by(peaks, masses, block_key, key_count)
    maxima, totals = joined((maxima, totals), "rep", merge_logsum)
    return -EPSILON * (maxima + jnp.log(totals))


def settle_targets(maxima, totals, half_blocks):
    lower_row = lax.axis_index("rep") * half_blocks
    maxima_half = lax.dynamic_slice_in_dim(maxima, lower_row, half_blocks, 0)
    totals_half = lax.dynamic_slice_in_dim(totals, lower_row, half_blocks, 0)
    dual_half = -EPSILON * (maxima_half + jnp.log(totals_half))
    return lax.all_gather(dual_half, "rep", axis=0, tiled=True)


def owner_pairs(asked_ids):
    ranking = jnp.argsort(jnp.where(asked_ids >= 0, 0, 1), stable=True)
    pair_total = jnp.sum((asked_ids >= 0).astype(jnp.int32))
    return (ranking, jnp.maximum(asked_ids[ranking], 0), pair_total)


def collect_by(partials, masses, block_key, key_count):
    member = (block_key[:, None] == jnp.arange(key_count)[None, :]).astype(jnp.float32)
    numerator = jnp.einsum("sb,sjd->bjd", member, partials, precision=lax.Precision.HIGHEST)
    column_mass = jnp.einsum("sb,sj->bj", member, masses, precision=lax.Precision.HIGHEST)
    return (numerator, column_mass)


def on_device(src_points, tgt_points, pair_source, pair_target, pair_count):
    peer_count = lax.axis_size("pts")
    point_rows, feat_width = src_points.shape
    block_len = BLOCK
    blocks = point_rows // block_len
    half_blocks = blocks // lax.axis_size("rep")
    own_sources = src_points.reshape(blocks, block_len, feat_width)
    own_targets = tgt_points.reshape(blocks, block_len, feat_width)
    source_sq = squares(own_sources)
    target_sq = squares(own_targets)
    pair_total = pair_count[0]
    slot_total = pair_source.shape[0]
    usable = jnp.arange(slot_total) < pair_total
    source_local = jnp.where(usable, pair_source % blocks, 0)
    owner_ids = jnp.where(usable, pair_target // blocks, 0)
    target_local = jnp.where(usable, pair_target % blocks, 0)
    matched = (owner_ids[:, None] == jnp.arange(peer_count)[None, :]) & usable[:, None]
    wanted = jnp.max(jnp.where(matched, target_local[:, None], -1), axis=0)
    source_of_owner = jnp.max(jnp.where(matched, source_local[:, None], -1), axis=0)
    served = source_of_owner >= 0
    source_index = jnp.maximum(source_of_owner, 0)
    outgoing = jnp.where(
        served[:, None, None], own_sources[source_index], jnp.zeros((), src_points.dtype)
    )
    asked_ids = lax.all_to_all(wanted, "pts", split_axis=0, concat_axis=0, tiled=True)
    replies = jnp.where(
        (asked_ids >= 0)[:, None, None],
        own_targets[jnp.maximum(asked_ids, 0)],
        jnp.zeros((), tgt_points.dtype),
    )
    fetched = lax.all_to_all(replies, "pts", split_axis=0, concat_axis=0, tiled=True)
    fetched_sq = squares(fetched)
    sweep_slots = (
        own_sources[source_local],
        source_sq[source_local],
        fetched[owner_ids],
        fetched_sq[owner_ids],
    )
    target_slices = jnp.zeros((peer_count, block_len), jnp.float32)
    owner_drop = jnp.where(usable, owner_ids, peer_count)
    for round_no in range(ITERS):
        peaks, masses = pair_sweep(
            sweep_slots,
            pair_total,
            row_visit(target_slices[owner_ids]),
            fresh_stats(slot_total, block_len),
        )
        source_dual = settle_sources(peaks, masses, jnp.where(usable, source_local, -1), blocks)
        peaks, masses = pair_sweep(
            sweep_slots,
            pair_total,
            column_visit(source_dual[source_local]),
            fresh_stats(slot_total, block_len),
        )
        out_peaks = (
            jnp.full((peer_count, block_len), NEG_BIG, jnp.float32)
            .at[owner_drop]
            .set(peaks, mode="drop")
        )
        out_masses = (
            jnp.zeros((peer_count, block_len), jnp.float32).at[owner_drop].set(masses, mode="drop")
        )
        in_peaks, in_masses = (
            lax.all_to_all(out_peaks, "pts", split_axis=0, concat_axis=0, tiled=True),
            lax.all_to_all(out_masses, "pts", split_axis=0, concat_axis=0, tiled=True),
        )
        maxima, totals = combine_by(in_peaks, in_masses, asked_ids, blocks)
        target_dual = settle_targets(maxima, totals, half_blocks)
        if round_no + 1 < ITERS:
            returned = jnp.where(
                (asked_ids >= 0)[:, None], target_dual[jnp.maximum(asked_ids, 0)], 0.0
            )
            target_slices = lax.all_to_all(returned, "pts", split_axis=0, concat_axis=0, tiled=True)
    received = lax.all_to_all(outgoing, "pts", split_axis=0, concat_axis=0, tiled=True)
    sent_duals = jnp.where(served[:, None], source_dual[source_index], 0.0)
    received_duals = lax.all_to_all(sent_duals, "pts", split_axis=0, concat_axis=0, tiled=True)
    ranking, target_pick, received_total = owner_pairs(asked_ids)
    received_sq = squares(received)
    owner_slots = (
        received[ranking],
        received_sq[ranking],
        own_targets[target_pick],
        target_sq[target_pick],
    )
    start_sums = (
        jnp.zeros((peer_count, block_len, feat_width), jnp.float32),
        jnp.zeros((peer_count, block_len), jnp.float32),
    )
    partials, masses = pair_sweep(
        owner_slots,
        received_total,
        gradient_visit(received_duals[ranking], target_dual[target_pick]),
        start_sums,
    )
    gradient_key = jnp.where(jnp.arange(peer_count) < received_total, target_pick, -1)
    numerator, column_mass = collect_by(partials, masses, gradient_key, blocks)
    lower_row = lax.axis_index("rep") * half_blocks
    target_half = lax.dynamic_slice_in_dim(own_targets, lower_row, half_blocks, 0).astype(
        jnp.float32
    )
    mass_half = lax.dynamic_slice_in_dim(column_mass, lower_row, half_blocks, 0)
    numerator_half = lax.dynamic_slice_in_dim(numerator, lower_row, half_blocks, 0)
    gradient_half = target_half * mass_half[:, :, None] - numerator_half
    gradient = lax.all_gather(gradient_half, "rep", axis=0, tiled=True)
    return (
        source_dual.reshape(-1),
        target_dual.reshape(-1),
        gradient.reshape(blocks * block_len, feat_width),
    )


def solution(mesh):
    return jax.shard_map(
        on_device,
        mesh=mesh,
        in_specs=(
            P("pts", None),
            P("pts", None),
            P(("pts", "rep")),
            P(("pts", "rep")),
            P(("pts", "rep")),
        ),
        out_specs=(P("pts"), P("pts"), P("pts", None)),
        check_vma=False,
    )
```

profile of v0, /device:TPU:1, one launch (start us, length us, event | category | flops | bytes accessed | tf_op | source)
XLA Modules:
  0.0 961.9 jit_solution(4892562002878372125)
XLA Ops:
  9.4 26.7 %all_to_all.103 = s32[128,1,1]{2,1,0:T(1,128)S(1)} all-to-all(s32[128,1,1]{2,1,0:T(1,128)S(1)} %copy.53), channel_id=1, replica_groups=mesh['pts'=128,'rep'=2] {'pts'}, dimensions={0} | all-to-all | bytes 1024 | tf_op jit(solution)/shard_map/all_to_all | solution.py:180
  36.1 4.7 fusion.97
  40.8 7.9 gather_fusion.2
  48.7 2.4 compare_reduce_fusion
  51.0 7.2 broadcast_select_fusion.1
  58.3 7.9 all-to-all-start.1
  67.3 6.0 gather_fusion.4
  74.1 175.4 %all-to-all-done.1 = bf16[128,128,256]{2,1,0:T(8,128)(2,1)} async-done(((bf16[128,128,256]{2,1,0:T(8,128)(2,1)}), bf16[128,128,256]{2,1,0:T(8,128)(2,1)}, u32[]{:S(2)}, u32[]{:S(2)}) %all-to-all-start.1) | async-done | bytes 8388640 | tf_op jit(solution)/shard_map/all_to_all | solution.py:186
  249.5 5.6 multiply_reduce_fusion.1
  255.8 9.4 gather_fusion.5
  265.2 29.1 %while.31 = (s32[]{:T(128)}, f32[96,128]{1,0:T(8,128)S(1)}, f32[96,128]{1,0:T(8,128)S(1)}, s32[]{:T(128)}, s32[]{:T(128)}, /*index=5*/f32[96,128]{1,0:T(8,128)S(...) while((s32[]{:T(128)}, f32[96,128]{1,0:T(8,128)S(1)}, ...), condition=%wide.region_6.7_spmd, body=%wide.region_3.6_spmd.sunk | while | flops 68288536 | bytes 2164439 | solution.py:49
  294.7 1.8 all-gather
  297.1 1.8 all-gather.1
  299.6 29.1 %while.32 = (s32[]{:T(128)}, f32[96,128]{1,0:T(8,128)S(1)}, f32[96,128]{1,0:T(8,128)S(1)}, s32[]{:T(128)}, s32[]{:T(128)}, /*index=5*/f32[96,128]{1,0:T(8,128)S(...) while((s32[]{:T(128)}, f32[96,128]{1,0:T(8,128)S(1)}, ...), condition=%wide.region_12.13_spmd, body=%wide.region_9.12_spmd.sunk | while | flops 68288536 | bytes 2164439 | solution.py:49
  330.0 7.5 all-to-all-start.2
  338.9 9.1 all-to-all-done.2
  348.0 6.5 all-to-all-start.3
  355.1 10.0 %all-to-all-done.3 = f32[128,1,128]{2,1,0:T(1,128)S(1)} async-done(((f32[128,1,128]{2,1,0:T(1,128)}), f32[128,1,128]{2,1,0:T(1,128)S(1)}, u32[]{:S(2)}, u32[]{:S(2)}) %all-to-all-start.3) | async-done | bytes 65568 | tf_op jit(solution)/shard_map/all_to_all | solution.py:220
  365.8 4.5 all-gather.6
  371.7 6.2 all-to-all-start.4
  377.9 6.6 gather_fusion.17
  384.5 3.9 all-to-all-done.4
  389.1 29.1 %while.33 = (s32[]{:T(128)}, f32[96,128]{1,0:T(8,128)S(1)}, f32[96,128]{1,0:T(8,128)S(1)}, s32[]{:T(128)}, s32[]{:T(128)}, /*index=5*/f32[96,128]{1,0:T(8,128)S(...) while((s32[]{:T(128)}, f32[96,128]{1,0:T(8,128)S(1)}, ...), condition=%wide.region_20.21_spmd, body=%wide.region_17.20_spmd.sunk | while | flops 68288536 | bytes 2164439 | solution.py:49
  418.6 1.8 all-gather.2
  420.9 1.8 all-gather.3
  423.4 29.1 %while.34 = (s32[]{:T(128)}, f32[96,128]{1,0:T(8,128)S(1)}, f32[96,128]{1,0:T(8,128)S(1)}, s32[]{:T(128)}, s32[]{:T(128)}, /*index=5*/f32[96,128]{1,0:T(8,128)S(...) while((s32[]{:T(128)}, f32[96,128]{1,0:T(8,128)S(1)}, ...), condition=%wide.region_26.27_spmd, body=%wide.region_23.26_spmd.sunk | while | flops 68288536 | bytes 2164439 | solution.py:49
  453.9 7.3 all-to-all-start.5
  462.6 9.1 all-to-all-done.5
  471.7 6.1 all-to-all-start.6
  477.9 7.3 broadcast_select_fusion
  485.2 3.4 all-to-all-done.6
  488.6 10.7 %all-to-all-start.11 = ((bf16[128,128,256]{2,1,0:T(8,128)(2,1)}), bf16[128,128,256]{2,1,0:T(8,128)(2,1)}, u32[]{:S(2)}, u32[]{:S(2)}) async-start(bf16[128,128,256]{2,1,0:T(8,128)(2,1)} %broadcast_select_fusion), calls=%async_computation.11 | async-start | bytes 16777216 | tf_op jit(solution)/shard_map/all_to_all | solution.py:229
  502.1 2.6 sort.17
  506.6 6.5 gather_fusion.21
  515.1 1.8 all-gather.7
  518.2 161.9 %all-to-all-done.11 = bf16[128,128,256]{2,1,0:T(8,128)(2,1)} async-done(((bf16[128,128,256]{2,1,0:T(8,128)(2,1)}), bf16[128,128,256]{2,1,0:T(8,128)(2,1)}, u32[]{:S(2)}, u32[]{:S(2)}) %all-to-all-start.11) | async-done | bytes 8388640 | tf_op jit(solution)/shard_map/all_to_all | solution.py:229
  680.2 12.8 %all-to-all-start.7 = ((f32[128,1,128]{2,1,0:T(1,128)}), f32[128,1,128]{2,1,0:T(1,128)S(1)}, u32[]{:S(2)}, u32[]{:S(2)}) async-start(f32[128,1,128]{2,1,0:T(1,128)} %bitcast.22), calls=%async_computation.7 | async-start | bytes 131072 | tf_op jit(solution)/shard_map/all_to_all | solution.py:228
  693.0 5.6 multiply_reduce_fusion
  699.3 10.0 %gather_fusion.20 = bf16[128,128,256]{2,1,0:T(8,128)(2,1)} fusion(bf16[128,128,256]{2,1,0:T(8,128)(2,1)} %all-to-all-done.11, s32[1024]{0:T(1024)S(1)} %pad_clamp_fusion.2), kind=kCustom, calls=%fused_computation.20 | custom fusion | bytes 16777728 | tf_op jit(solution)/shard_map/gather | solution.py:235
  710.0 29.1 %while.106 = (s32[]{:T(128)}, f32[96,128]{1,0:T(8,128)S(1)}, f32[96,128]{1,0:T(8,128)S(1)}, s32[]{:T(128)}, s32[]{:T(128)}, /*index=5*/f32[96,128]{1,0:T(8,128)S...) while((s32[]{:T(128)}, f32[96,128]{1,0:T(8,128)S(1)}, ...), condition=%wide.region_34.35_spmd, body=%wide.region_31.34_spmd.sunk | while | flops 68288536 | bytes 2164439 | solution.py:49
  739.5 2.0 all-gather.4
  742.1 1.8 all-gather.5
  745.2 29.1 %while.107 = (s32[]{:T(128)}, f32[96,128]{1,0:T(8,128)S(1)}, f32[96,128]{1,0:T(8,128)S(1)}, s32[]{:T(128)}, s32[]{:T(128)}, /*index=5*/f32[96,128]{1,0:T(8,128)S...) while((s32[]{:T(128)}, f32[96,128]{1,0:T(8,128)S(1)}, ...), condition=%wide.region_40.41_spmd, body=%wide.region_37.40_spmd.sunk | while | flops 68288536 | bytes 2164439 | solution.py:49
  775.6 11.2 %all-to-all-start.8 = ((f32[128,1,128]{2,1,0:T(1,128)}), f32[128,1,128]{2,1,0:T(1,128)S(1)}, u32[]{:S(2)}, u32[]{:S(2)}) async-start(f32[128,1,128]{2,1,0:T(1,128)} %bitcast.29), calls=%async_computation.8 | async-start | bytes 131072 | tf_op jit(solution)/shard_map/all_to_all | solution.py:219
  788.9 8.6 all-to-all-done.8
  797.5 6.1 all-to-all-start.9
  804.2 10.0 %all-to-all-done.9 = f32[128,1,128]{2,1,0:T(1,128)S(1)} async-done(((f32[128,1,128]{2,1,0:T(1,128)}), f32[128,1,128]{2,1,0:T(1,128)S(1)}, u32[]{:S(2)}, u32[]{:S(2)}) %all-to-all-start.9) | async-done | bytes 65568 | tf_op jit(solution)/shard_map/all_to_all | solution.py:220
  814.3 6.1 all-to-all-start.10
  821.1 2.7 all-gather.8
  823.8 7.1 all-to-all-done.10
  832.2 7.8 broadcast_in_dim.483.clone
  840.1 43.1 %while.108 = (s32[]{:T(128)}, f32[128,128,256]{2,0,1:T(8,128)}, f32[128,128]{1,0:T(8,128)S(1)}, s32[]{:T(128)}, s32[]{:T(128)}, /*index=5*/f32[128,128]{1,0:T(8,...) while((s32[]{:T(128)}, f32[128,128,256]{2,0,1:T(8,128)}, ...), condition=%wide.region_52.53_spmd, body=%wide.region_50.52_spmd.sunk | while | flops 135527456 | bytes 5305583 | solution.py:49
  840.8 1.6 fusion.128
  849.1 1.7 copy_dynamic-update-slice_fusion.2
  856.8 1.6 fusion.128
  859.8 1.6 copy_dynamic-update-slice_fusion.2
  870.5 1.7 copy_dynamic-update-slice_fusion.2
  875.9 1.7 copy_dynamic-update-slice_fusion.2
  881.3 1.7 copy_dynamic-update-slice_fusion.2
  883.2 9.1 fusion.89
  892.5 1.9 dynamic-slice_subtract_fusion
  894.4 2.1 copy.65
  897.7 53.1 %all-gather.11.cloned.1.call-done = f32[24,128,256]{2,1,0:T(8,128)} async-done(((f32[12,128,256]{2,1,0:T(8,128)}), f32[24,128,256]{2,1,0:T(8,128)}) %all-gather.11.cloned.1.call-update) | async-done | bytes 3145744 | tf_op jit(solution)/shard_map/all_gather | solution.py:259
  950.9 3.8 copy.169
  (576 shorter events, 238.2 us)
Async XLA Ops:
  58.3 7.9 copy-start.1
  58.3 191.3 %all-to-all-start.1 = ((bf16[128,128,256]{2,1,0:T(8,128)(2,1)}), bf16[128,128,256]{2,1,0:T(8,128)(2,1)}, u32[]{:S(2)}, u32[]{:S(2)}) async-start(bf16[128,128,256]{2,1,0:T(8,128)(2,1)} %broadcast_select_fusion.1), calls=%async_computation.1 | async-start | bytes 16777216 | tf_op jit(solution)/shard_map/all_to_all | solution.py:186
  330.0 18.0 %all-to-all-start.2 = ((f32[128,1,128]{2,1,0:T(1,128)}), f32[128,1,128]{2,1,0:T(1,128)S(1)}, u32[]{:S(2)}, u32[]{:S(2)}) async-start(f32[128,1,128]{2,1,0:T(1,128)} %bitcast.5), calls=%async_computation.2 | async-start | bytes 131072 | tf_op jit(solution)/shard_map/all_to_all | solution.py:219
  348.0 17.1 %all-to-all-start.3 = ((f32[128,1,128]{2,1,0:T(1,128)}), f32[128,1,128]{2,1,0:T(1,128)S(1)}, u32[]{:S(2)}, u32[]{:S(2)}) async-start(f32[128,1,128]{2,1,0:T(1,128)} %bitcast.8), calls=%async_computation.3 | async-start | bytes 131072 | tf_op jit(solution)/shard_map/all_to_all | solution.py:220
  371.7 16.7 %all-to-all-start.4 = ((f32[128,1,128]{2,1,0:T(1,128)}), f32[128,1,128]{2,1,0:T(1,128)S(1)}, u32[]{:S(2)}, u32[]{:S(2)}) async-start(f32[128,1,128]{2,1,0:T(1,128)} %bitcast.12), calls=%async_computation.4 | async-start | bytes 131072 | tf_op jit(solution)/shard_map/all_to_all | solution.py:228
  453.9 17.9 %all-to-all-start.5 = ((f32[128,1,128]{2,1,0:T(1,128)}), f32[128,1,128]{2,1,0:T(1,128)S(1)}, u32[]{:S(2)}, u32[]{:S(2)}) async-start(f32[128,1,128]{2,1,0:T(1,128)} %bitcast.15), calls=%async_computation.5 | async-start | bytes 131072 | tf_op jit(solution)/shard_map/all_to_all | solution.py:219
  471.7 16.8 %all-to-all-start.6 = ((f32[128,1,128]{2,1,0:T(1,128)}), f32[128,1,128]{2,1,0:T(1,128)S(1)}, u32[]{:S(2)}, u32[]{:S(2)}) async-start(f32[128,1,128]{2,1,0:T(1,128)} %bitcast.18), calls=%async_computation.6 | async-start | bytes 131072 | tf_op jit(solution)/shard_map/all_to_all | solution.py:220
  485.2 14.1 %copy-start = (bf16[3072,256]{1,0:T(8,128)(2,1)S(1)}, bf16[3072,256]{1,0:T(8,128)(2,1)}, u32[]{:S(2)}) copy-start(bf16[3072,256]{1,0:T(8,128)(2,1)} %param.20) | copy-start | bytes 4718596
  488.6 191.6 %all-to-all-start.11 = ((bf16[128,128,256]{2,1,0:T(8,128)(2,1)}), bf16[128,128,256]{2,1,0:T(8,128)(2,1)}, u32[]{:S(2)}, u32[]{:S(2)}) async-start(bf16[128,128,256]{2,1,0:T(8,128)(2,1)} %broadcast_select_fusion), calls=%async_computation.11 | async-start | bytes 16777216 | tf_op jit(solution)/shard_map/all_to_all | solution.py:229
  680.2 29.1 %all-to-all-start.7 = ((f32[128,1,128]{2,1,0:T(1,128)}), f32[128,1,128]{2,1,0:T(1,128)S(1)}, u32[]{:S(2)}, u32[]{:S(2)}) async-start(f32[128,1,128]{2,1,0:T(1,128)} %bitcast.22), calls=%async_computation.7 | async-start | bytes 131072 | tf_op jit(solution)/shard_map/all_to_all | solution.py:228
  775.6 21.9 %all-to-all-start.8 = ((f32[128,1,128]{2,1,0:T(1,128)}), f32[128,1,128]{2,1,0:T(1,128)S(1)}, u32[]{:S(2)}, u32[]{:S(2)}) async-start(f32[128,1,128]{2,1,0:T(1,128)} %bitcast.29), calls=%async_computation.8 | async-start | bytes 131072 | tf_op jit(solution)/shard_map/all_to_all | solution.py:219
  797.5 16.7 %all-to-all-start.9 = ((f32[128,1,128]{2,1,0:T(1,128)}), f32[128,1,128]{2,1,0:T(1,128)S(1)}, u32[]{:S(2)}, u32[]{:S(2)}) async-start(f32[128,1,128]{2,1,0:T(1,128)} %bitcast.32), calls=%async_computation.9 | async-start | bytes 131072 | tf_op jit(solution)/shard_map/all_to_all | solution.py:220
  814.3 16.7 %all-to-all-start.10 = ((f32[128,1,128]{2,1,0:T(1,128)}), f32[128,1,128]{2,1,0:T(1,128)S(1)}, u32[]{:S(2)}, u32[]{:S(2)}) async-start(f32[128,1,128]{2,1,0:T(1,128)} %bitcast.36), calls=%async_computation.10 | async-start | bytes 131072 | tf_op jit(solution)/shard_map/all_to_all | solution.py:231
  820.4 130.5 %all-gather.11.cloned.1.call-start = ((), (), s32[]{:S(2)}) async-start(), calls=%async_computation.12 | async-start | bytes 4718592 | tf_op jit(solution)/shard_map/all_gather | solution.py:259
Sparse Core Ops, SparseCore 0:
  896.6 54.1 all-gather.10
where the time goes:
time: 974 us; the launch traced here: 962 us
  waiting for transfers between devices  452 us (46%)
  matrix products  147 us (15%)
  other arithmetic  115 us (12%)
  local copies, waits for them, and re-layouts  94.5 us (10%)
  starting transfers between devices  88.4 us (9%)
  blocking collectives  47 us (5%)
  between operations  16.3 us (2%)
    all_to_all x1, waiting for transfers between devices, on_device(): lax.all_to_all(replies, 'pts', split_axis=0, concat_axis=0, tiled=True)  175 us
    all_to_all x1, waiting for transfers between devices, on_device(): lax.all_to_all(outgoing, 'pts', split_axis=0, concat_axis=0, tiled=True)  162 us
    dot_general x80, matrix products, pair_costs(): jnp.einsum('gid,gjd->gij', source_rows, target_rows, preferred_element_ty...  126 us
    all_gather x1, waiting for transfers between devices, on_device(): gradient = lax.all_gather(gradient_half, 'rep', axis=0, tiled=True)  53.1 us
    lt x80, other arithmetic, advance(): in_use = first_row + jnp.arange(8) < pair_total  52.5 us
    all_to_all x3, waiting for transfers between devices, on_device(): lax.all_to_all(out_peaks, 'pts', split_axis=0, concat_axis=0, tiled=True)  26.8 us
    all_to_all x1, blocking collectives, on_device(): lax.all_to_all(wanted, 'pts', split_axis=0, concat_axis=0, tiled=True)  26.7 us
    all_to_all x3, starting transfers between devices, on_device(): lax.all_to_all(out_peaks, 'pts', split_axis=0, concat_axis=0, tiled=True)  26 us
  transfers between devices with their start and end apart: 12, of which 11 were waited for; matrix products, arithmetic and copies ran while one was open for 6% of the time, Pallas kernels for 0%

commit v1 on v0

v1 whole, which is shorter than its diff:
```python
import jax
import jax.numpy as jnp
from jax import lax
from jax.sharding import PartitionSpec as P

BLOCK = 128
ITERS = 3


EPSILON = 0.05
NEG_BIG = -1e30


def squares(blocks_in):
    return jnp.sum(jnp.square(blocks_in.astype(jnp.float32)), axis=-1)


def pair_costs(source_rows, target_rows):
    inner_dot = jnp.einsum(
        "gid,gjd->gij", source_rows, target_rows, preferred_element_type=jnp.float32
    )
    source_sq = squares(source_rows)
    target_sq = squares(target_rows)
    return (source_sq[:, :, None] + target_sq[:, None, :] - 2.0 * inner_dot) / source_rows.shape[2]


def pair_lse(scores, axis):
    peaks = jnp.max(scores, axis=axis)
    masses = jnp.sum(jnp.exp(scores - jnp.expand_dims(peaks, axis)), axis=axis)
    return peaks + jnp.log(masses)


def combine_by(values, block_key, key_count):
    member = (block_key[:, None] == jnp.arange(key_count)[None, :])[:, :, None]
    maxima = jnp.max(jnp.where(member, values[:, None, :], NEG_BIG), axis=0)
    shifts = jnp.where(member, values[:, None, :] - maxima[None, :, :], NEG_BIG)
    totals = jnp.sum(jnp.where(member, jnp.exp(shifts), 0.0), axis=0)
    return maxima, totals


def swap_rep(value):
    return lax.ppermute(value, "rep", [(0, 1), (1, 0)])


def a2a(value):
    return lax.all_to_all(value, "pts", split_axis=0, concat_axis=0, tiled=True)


def on_device(src_points, tgt_points, pair_source, pair_target, pair_count):
    peer_count = lax.axis_size("pts")
    point_rows, feat_width = src_points.shape
    block_len = BLOCK
    blocks = point_rows // block_len
    half_blocks = blocks // lax.axis_size("rep")
    rep_index = lax.axis_index("rep")
    lower_block = rep_index * half_blocks
    own_sources = src_points.reshape(blocks, block_len, feat_width)
    own_targets = tgt_points.reshape(blocks, block_len, feat_width)

    pair_total = pair_count[0]
    slot_total = pair_source.shape[0]
    usable = jnp.arange(slot_total) < pair_total
    source_local = jnp.where(usable, pair_source % blocks, 0)
    owner_ids = jnp.where(usable, pair_target // blocks, 0)
    target_local = jnp.where(usable, pair_target % blocks, 0)
    matched = (owner_ids[:, None] == jnp.arange(peer_count)[None, :]) & usable[:, None]
    wanted = jnp.max(jnp.where(matched, target_local[:, None], -1), axis=0)
    source_of_owner = jnp.max(jnp.where(matched, source_local[:, None], -1), axis=0)
    served = source_of_owner >= 0
    source_index = jnp.maximum(source_of_owner, 0)
    outgoing = jnp.where(
        served[:, None, None], own_sources[source_index], jnp.zeros((), src_points.dtype)
    )
    asked_ids = a2a(wanted)
    received = a2a(outgoing)

    valid = asked_ids >= 0
    half_key = jnp.where(valid, asked_ids - lower_block, -1)
    half_pick = jnp.clip(half_key, 0, half_blocks - 1)
    own_half = lax.dynamic_slice_in_dim(own_targets, lower_block, half_blocks, 0)
    pair_targets = own_half[half_pick]
    cost_grid = pair_costs(received, pair_targets)

    target_half = jnp.zeros((half_blocks, block_len), jnp.float32)
    for round_no in range(ITERS):
        target_here = target_half[half_pick]
        row_lse = pair_lse((target_here[:, None, :] - cost_grid) / EPSILON, 2)
        row_back = a2a(row_lse)
        maxima, totals = combine_by(row_back, source_of_owner, blocks)
        other_maxima, other_totals = swap_rep((maxima, totals))
        merged = jnp.maximum(maxima, other_maxima)
        merged_totals = totals * jnp.exp(maxima - merged) + other_totals * jnp.exp(
            other_maxima - merged
        )
        source_dual = -EPSILON * (merged + jnp.log(merged_totals))
        sent_duals = jnp.where(served[:, None], source_dual[source_index], 0.0)
        source_here = a2a(sent_duals)
        column_lse = pair_lse((source_here[:, :, None] - cost_grid) / EPSILON, 1)
        col_max, col_tot = combine_by(column_lse, half_key, half_blocks)
        target_half = -EPSILON * (col_max + jnp.log(col_tot))

    target_here = target_half[half_pick]
    plan = jnp.exp((source_here[:, :, None] + target_here[:, None, :] - cost_grid) / EPSILON)
    plan = jnp.where(valid[:, None, None], plan, 0.0)
    partial_value = jnp.einsum(
        "gij,gid->gjd",
        plan.astype(jnp.bfloat16),
        received,
        preferred_element_type=jnp.float32,
    )
    member = (half_key[:, None] == jnp.arange(half_blocks)[None, :]).astype(jnp.float32)
    numerator = jnp.einsum("sb,sjd->bjd", member, partial_value, precision=lax.Precision.HIGHEST)
    column_mass = jnp.einsum(
        "sb,sj->bj", member, jnp.sum(plan, axis=1), precision=lax.Precision.HIGHEST
    )
    gradient_half = own_half.astype(jnp.float32) * column_mass[:, :, None] - numerator
    target_dual = lax.all_gather(target_half, "rep", axis=0, tiled=True)
    gradient = lax.all_gather(gradient_half, "rep", axis=0, tiled=True)
    return (
        source_dual.reshape(-1),
        target_dual.reshape(-1),
        gradient.reshape(blocks * block_len, feat_width),
    )


def solution(mesh):
    return jax.shard_map(
        on_device,
        mesh=mesh,
        in_specs=(
            P("pts", None),
            P("pts", None),
            P(("pts", "rep")),
            P(("pts", "rep")),
            P(("pts", "rep")),
        ),
        out_specs=(P("pts"), P("pts"), P("pts", None)),
        check_vma=False,
    )
```

time: 974 us -> 512 us (0.53)
  waiting for transfers between devices: 452 us -> 205 us
  matrix products: 147 us -> 42.1 us
  local copies, waits for them, and re-layouts: 94.5 us -> 27.8 us
  starting transfers between devices: 88.4 us -> 63.3 us
  other arithmetic: 115 us -> 101 us
    all_to_all x11 -> x5, waiting for transfers between devices: 399 us -> 193 us  [a2a(): return lax.all_to_all(value, 'pts', split_axis=0, concat_axis=0, tiled=True)]
    dot_general x80 -> x1, matrix products: 126 us -> 9.51 us  [pair_costs(): jnp.einsum('gid,gjd->gij', source_rows, target_rows, preferred_element_ty...]
    lt x80 -> x0, other arithmetic: 52.5 us -> none  [advance(): in_use = first_row + jnp.arange(8) < pair_total]
    all_gather x1, waiting for transfers between devices: 53.1 us -> 8.54 us  [on_device(): gradient = lax.all_gather(gradient_half, 'rep', axis=0, tiled=True)]
    gather x20 -> x5, local copies, waits for them, and re-layouts: 49.9 us -> 8.95 us  [the longest x1 6.37 us: on_device(): pair_targets = own_half[half_pick]]
    all_to_all x11 -> x5, starting transfers between devices: 88.4 us -> 53.7 us  [a2a(): return lax.all_to_all(value, 'pts', split_axis=0, concat_axis=0, tiled=True)]
    reduce_sum x78 -> x13, other arithmetic: 9.8 us -> 42.5 us  [the longest x6 34 us: pair_lse(): masses = jnp.sum(jnp.exp(scores - jnp.expand_dims(peaks, axis)), axis=axis)]
    reduce_max x6 -> x11, other arithmetic: 3.05 us -> 30 us  [the longest x5 27.5 us: pair_lse(): peaks = jnp.max(scores, axis=axis)]
  transfers between devices with their start and end apart: 12 -> 12, of which waited for: 11 -> 11; matrix products, arithmetic and copies ran while one was open for 6% -> 7% of each run, Pallas kernels for 0% -> 0%
where the time goes in v1:
time: 512 us; the launch traced here: 506 us
  waiting for transfers between devices  205 us (40%)
  other arithmetic  101 us (20%)
  starting transfers between devices  63.3 us (12%)
  blocking collectives  51.5 us (10%)
  matrix products  42.1 us (8%)
  local copies, waits for them, and re-layouts  27.8 us (5%)
  between operations  15.4 us (3%)
    all_to_all x5, waiting for transfers between devices, a2a(): return lax.all_to_all(value, 'pts', split_axis=0, concat_axis=0, tiled=True)  193 us
    all_to_all x5, starting transfers between devices, a2a(): return lax.all_to_all(value, 'pts', split_axis=0, concat_axis=0, tiled=True)  53.7 us
    all_to_all x3, blocking collectives, a2a(): return lax.all_to_all(value, 'pts', split_axis=0, concat_axis=0, tiled=True)  48.7 us
    reduce_sum x6, other arithmetic, pair_lse(): masses = jnp.sum(jnp.exp(scores - jnp.expand_dims(peaks, axis)), axis=axis)  34 us
    reduce_max x5, other arithmetic, pair_lse(): peaks = jnp.max(scores, axis=axis)  27.5 us
    dot_general x1, matrix products, on_device(): jnp.einsum('sb,sjd->bjd', member, partial_value, precision=lax.Precision....  20.6 us
    dot_general x1, matrix products, on_device(): jnp.einsum('gij,gid->gjd', plan.astype(jnp.bfloat16), received, preferred...  11.8 us
    reduce_sum x2, other arithmetic, squares(): return jnp.sum(jnp.square(blocks_in.astype(jnp.float32)), axis=-1)  11.2 us
  transfers between devices with their start and end apart: 12, of which 11 were waited for; matrix products, arithmetic and copies ran while one was open for 7% of the time, Pallas kernels for 0%

profile of v1, /device:TPU:1, one launch (start us, length us, event | category | flops | bytes accessed | tf_op | source)
XLA Modules:
  0.0 506.4 jit_solution(17960676834219262913)
XLA Ops:
  8.0 0.7 fusion.31
  8.8 0.7 copy.38
  9.5 16.3 %all-to-all-start = ((s32[128,1,1]{2,1,0:T(1,128)}), s32[128,1,1]{2,1,0:T(1,128)S(1)}, u32[]{:S(2)}, u32[]{:S(2)}) async-start(s32[128,1,1]{2,1,0:T(1,128)} %copy.38), calls=%async_computation | async-start | bytes 131072 | tf_op jit(solution)/shard_map/all_to_all | solution.py:46
  25.9 6.4 %gather_fusion.1 = bf16[128,128,256]{2,1,0:T(8,128)(2,1)} fusion(bf16[24,128,256]{2,1,0:T(8,128)(2,1)S(1)} %bitcast.38, s32[1024]{0:T(1024)S(1)} %pad_clamp_fusion), kind=kCustom, calls=%fused_computation.1 | custom fusion | bytes 16777728 | tf_op jit(solution)/shard_map/gather | solution.py:72
  32.3 7.2 %broadcast_select_fusion = bf16[128,128,256]{2,1,0:T(8,128)(2,1)} fusion(bf16[128,128,256]{2,1,0:T(8,128)(2,1)} %gather_fusion.1, pred[128]{0:T(512)(128)(4,1)S(1)} %broadcast_compare_fusion), kind=kLoop, calls=%fused_computation.27 | loop fusion | flops 4194304 | bytes 16777344 | tf_op jit(solution)/shard_map/jit(_where)/select_n | solution.py:71
  39.5 14.2 %all-to-all-start.1 = ((bf16[128,128,256]{2,1,0:T(8,128)(2,1)}), bf16[128,128,256]{2,1,0:T(8,128)(2,1)}, u32[]{:S(2)}, u32[]{:S(2)}) async-start(bf16[128,128,256]{2,1,0:T(8,128)(2,1)} %broadcast_select_fusion), calls=%async_computation.1 | async-start | bytes 16777216 | tf_op jit(solution)/shard_map/all_to_all | solution.py:46
  53.8 4.6 fusion.36
  58.5 0.6 gather_fusion
  59.1 6.4 %gather_fusion.2 = bf16[128,128,256]{2,1,0:T(8,128)(2,1)} fusion(bf16[12,128,256]{2,1,0:T(8,128)(2,1)S(1)} %constant_dynamic-slice_fusion, s32[1024]{0:T(1024)S(1)} %pad_clamp_fusion.1), kind=kCustom, calls=%fused_computation.2 | custom fusion | bytes 16777728 | tf_op jit(solution)/shard_map/gather | solution.py:81
  65.5 5.6 %multiply_reduce_fusion = f32[128,128]{1,0:T(8,128)S(1)} fusion(bf16[128,128,256]{2,1,0:T(8,128)(2,1)} %gather_fusion.2), kind=kLoop, calls=%fused_computation.11 | loop fusion | flops 12566528 | bytes 8454144 | tf_op jit(solution)/shard_map/reduce_sum | solution.py:15
  71.1 164.5 %all-to-all-done.1 = bf16[128,128,256]{2,1,0:T(8,128)(2,1)} async-done(((bf16[128,128,256]{2,1,0:T(8,128)(2,1)}), bf16[128,128,256]{2,1,0:T(8,128)(2,1)}, u32[]{:S(2)}, u32[]{:S(2)}) %all-to-all-start.1) | async-done | bytes 8388640 | tf_op jit(solution)/shard_map/all_to_all | solution.py:46
  235.6 5.6 %multiply_reduce_fusion.1 = f32[128,128]{1,0:T(8,128)S(1)} fusion(bf16[128,128,256]{2,1,0:T(8,128)(2,1)} %all-to-all-done.1), kind=kLoop, calls=%fused_computation.12 | loop fusion | flops 12566528 | bytes 8454144 | tf_op jit(solution)/shard_map/reduce_sum | solution.py:15
  241.3 9.5 %fusion.2 = (f32[128,128]{1,0:T(8,128)S(1)}, f32[128,128,128]{2,1,0:T(8,128)S(1)}) fusion(f32[128,128]{1,0:T(8,128)S(1)} %gather_fusion, bf16[128,128,256]{2,1,0:T(8,128)(2,1)} %all-to-all-done.1, bf16[128,128,256]{2,1,0:T(8,128)(2,1)} %gather_fusion.2, f32[128,128]{1,0:T(8,128)S(1)} %multiply_reduce_fusion, f32[128,128]{1,0:T(8,128)S(1)} %multiply_reduce_fusion.1), kind=kOutput, calls=%fused_computation.28 | convolution fusion | flops 1088405504 | bytes 25427968 | tf_op jit(solution)/shard_map/gid,gjd->gij/dot_general | solution.py:19
  250.8 3.2 copy-done.2
  254.0 4.8 exponential_reduce_fusion.5
  258.8 0.6 log_add_fusion.5
  259.4 10.8 %all-to-all-start.2 = ((f32[128,1,128]{2,1,0:T(1,128)}), f32[128,1,128]{2,1,0:T(1,128)S(1)}, u32[]{:S(2)}, u32[]{:S(2)}) async-start(f32[128,1,128]{2,1,0:T(1,128)} %bitcast.5), calls=%async_computation.2 | async-start | bytes 131072 | tf_op jit(solution)/shard_map/all_to_all | solution.py:46
  270.3 10.4 %all-to-all-done.2 = f32[128,1,128]{2,1,0:T(1,128)S(1)} async-done(((f32[128,1,128]{2,1,0:T(1,128)}), f32[128,1,128]{2,1,0:T(1,128)S(1)}, u32[]{:S(2)}, u32[]{:S(2)}) %all-to-all-start.2) | async-done | bytes 65568 | tf_op jit(solution)/shard_map/all_to_all | solution.py:46
  280.7 0.6 select_reduce_fusion.5
  281.3 0.6 select_reduce_fusion.4
  281.9 3.5 collective-permute-start.1
  285.5 0.7 collective-permute-done.1
  286.6 0.6 gather_fusion.3
  287.2 0.7 bitcast_select_fusion.2
  287.9 6.3 %all-to-all-start.3 = ((f32[128,1,128]{2,1,0:T(1,128)}), f32[128,1,128]{2,1,0:T(1,128)S(1)}, u32[]{:S(2)}, u32[]{:S(2)}) async-start(f32[128,1,128]{2,1,0:T(1,128)} %bitcast.8), calls=%async_computation.3 | async-start | bytes 131072 | tf_op jit(solution)/shard_map/all_to_all | solution.py:46
  294.3 10.7 %all-to-all-done.3 = f32[128,1,128]{2,1,0:T(1,128)S(1)} async-done(((f32[128,1,128]{2,1,0:T(1,128)}), f32[128,1,128]{2,1,0:T(1,128)S(1)}, u32[]{:S(2)}, u32[]{:S(2)}) %all-to-all-start.3) | async-done | bytes 65568 | tf_op jit(solution)/shard_map/all_to_all | solution.py:46
  304.9 5.8 %fusion.3 = f32[128,128]{1,0:T(8,128)S(1)} fusion(f32[128,128,128]{2,1,0:T(8,128)} %copy-done.2, f32[128,128]{1,0:T(8,128)S(1)} %bitcast.46), kind=kLoop, calls=%fused_computation.29 | loop fusion | flops 6275072 | bytes 8519680 | tf_op jit(solution)/shard_map/reduce_max | solution.py:28
  310.9 4.9 exponential_reduce_fusion.4
  316.4 0.6 gather_fusion.4
  317.1 5.6 %fusion.4 = f32[128,128]{1,0:T(8,128)S(1)} fusion(f32[128,128,128]{2,1,0:T(8,128)} %copy-done.2, f32[128,128]{1,0:T(8,128)S(1)} %gather_fusion.4), kind=kLoop, calls=%fused_computation.30 | loop fusion | flops 6275072 | bytes 8519680 | tf_op jit(solution)/shard_map/reduce_max | solution.py:28
  322.7 6.8 %exponential_reduce_fusion.3 = f32[128,128]{1,0:T(8,128)S(1)} fusion(f32[128,128,128]{2,1,0:T(8,128)} %copy-done.2, f32[128,128]{1,0:T(8,128)S(1)} %fusion.4, f32[128,128]{1,0:T(8,128)S(1)} %gather_fusion.4), kind=kLoop, calls=%fused_computation.20 | loop fusion | flops 8372224 | bytes 8585216 | tf_op jit(solution)/shard_map/reduce_sum | solution.py:29
  329.6 16.1 %all_to_all.50 = f32[128,1,128]{2,1,0:T(1,128)S(1)} all-to-all(f32[128,1,128]{2,1,0:T(1,128)S(1)} %bitcast.51), channel_id=1, replica_groups=mesh['pts'=128,'rep'=2] {'pts'}, dimensions={0} | all-to-all | bytes 131072 | tf_op jit(solution)/shard_map/all_to_all | solution.py:46
  345.7 0.6 select_reduce_fusion.3
  346.3 0.6 select_reduce_fusion.2
  346.8 2.6 collective-permute-start.3
  349.5 0.7 collective-permute-done.3
  350.6 0.6 gather_fusion.5
  351.4 16.4 %all_to_all.51 = f32[128,1,128]{2,1,0:T(1,128)S(1)} all-to-all(f32[128,1,128]{2,1,0:T(1,128)S(1)} %bitcast.59), channel_id=1, replica_groups=mesh['pts'=128,'rep'=2] {'pts'}, dimensions={0} | all-to-all | bytes 131072 | tf_op jit(solution)/shard_map/all_to_all | solution.py:46
  367.8 5.2 %fusion.5 = f32[128,128]{1,0:T(8,128)S(1)} fusion(f32[128,128,128]{2,1,0:T(8,128)} %copy-done.2, f32[128,128]{1,0:T(8,128)S(1)} %bitcast.48), kind=kLoop, calls=%fused_computation.31 | loop fusion | flops 6275072 | bytes 8519680 | tf_op jit(solution)/shard_map/reduce_max | solution.py:28
  373.0 5.3 %exponential_reduce_fusion.2 = f32[128,128]{1,0:T(8,128)S(1)} fusion(f32[128,128,128]{2,1,0:T(8,128)} %copy-done.2, f32[128,128]{1,0:T(8,128)S(1)} %fusion.5, f32[128,128]{1,0:T(8,128)S(1)} %bitcast.49), kind=kLoop, calls=%fused_computation.18 | loop fusion | flops 8372224 | bytes 8585216 | tf_op jit(solution)/shard_map/reduce_sum | solution.py:29
  379.0 0.6 gather_fusion.6
  379.6 5.6 %fusion.6 = f32[128,128]{1,0:T(8,128)S(1)} fusion(f32[128,128,128]{2,1,0:T(8,128)} %copy-done.2, f32[128,128]{1,0:T(8,128)S(1)} %gather_fusion.6), kind=kLoop, calls=%fused_computation.32 | loop fusion | flops 6275072 | bytes 8519680 | tf_op jit(solution)/shard_map/reduce_max | solution.py:28
  385.3 6.8 %exponential_reduce_fusion.1 = f32[128,128]{1,0:T(8,128)S(1)} fusion(f32[128,128,128]{2,1,0:T(8,128)} %copy-done.2, f32[128,128]{1,0:T(8,128)S(1)} %fusion.6, f32[128,128]{1,0:T(8,128)S(1)} %gather_fusion.6), kind=kLoop, calls=%fused_computation.16 | loop fusion | flops 8372224 | bytes 8585216 | tf_op jit(solution)/shard_map/reduce_sum | solution.py:29
  392.1 16.1 %all_to_all.52 = f32[128,1,128]{2,1,0:T(1,128)S(1)} all-to-all(f32[128,1,128]{2,1,0:T(1,128)S(1)} %bitcast.52), channel_id=1, replica_groups=mesh['pts'=128,'rep'=2] {'pts'}, dimensions={0} | all-to-all | bytes 131072 | tf_op jit(solution)/shard_map/all_to_all | solution.py:46
  408.3 0.6 select_reduce_fusion.1
  408.8 0.6 select_reduce_fusion
  409.4 2.7 collective-permute-start.5
  412.2 0.7 collective-permute-done.5
  413.3 0.6 gather_fusion.7
  414.0 0.7 bitcast_select_fusion
  414.7 6.1 %all-to-all-start.7 = ((f32[128,1,128]{2,1,0:T(1,128)}), f32[128,1,128]{2,1,0:T(1,128)S(1)}, u32[]{:S(2)}, u32[]{:S(2)}) async-start(f32[128,1,128]{2,1,0:T(1,128)} %bitcast.19), calls=%async_computation.7 | async-start | bytes 131072 | tf_op jit(solution)/shard_map/all_to_all | solution.py:46
  421.3 2.4 compare_reduce_fusion
  423.6 7.7 %all-to-all-done.7 = f32[128,1,128]{2,1,0:T(1,128)S(1)} async-done(((f32[128,1,128]{2,1,0:T(1,128)}), f32[128,1,128]{2,1,0:T(1,128)S(1)}, u32[]{:S(2)}, u32[]{:S(2)}) %all-to-all-start.7) | async-done | bytes 65568 | tf_op jit(solution)/shard_map/all_to_all | solution.py:46
  431.4 5.2 %fusion.7 = f32[128,128]{1,0:T(8,128)S(1)} fusion(f32[128,128,128]{2,1,0:T(8,128)} %copy-done.2, f32[128,128]{1,0:T(8,128)S(1)} %bitcast.42), kind=kLoop, calls=%fused_computation.33 | loop fusion | flops 6275072 | bytes 8519680 | tf_op jit(solution)/shard_map/reduce_max | solution.py:28
  436.6 5.3 %exponential_reduce_fusion = f32[128,128]{1,0:T(8,128)S(1)} fusion(f32[128,128,128]{2,1,0:T(8,128)} %copy-done.2, f32[128,128]{1,0:T(8,128)S(1)} %fusion.7, f32[128,128]{1,0:T(8,128)S(1)} %bitcast.43), kind=kLoop, calls=%fused_computation.14 | loop fusion | flops 8372224 | bytes 8585216 | tf_op jit(solution)/shard_map/reduce_sum | solution.py:29
  442.6 0.6 gather_fusion.8
  443.2 5.8 %fusion.9 = f32[128,128]{1,0:T(8,128)S(1)} fusion(f32[128,128,128]{2,1,0:T(8,128)} %copy-done.2, f32[128,128]{1,0:T(8,128)S(1)} %gather_fusion.8, f32[128,128]{1,0:T(8,128)S(1)} %bitcast.44, pred[128]{0:T(512)(128)(4,1)S(1)} %compare_reduce_fusion), kind=kLoop, calls=%fused_computation.35 | loop fusion | flops 10469376 | bytes 8585344 | tf_op jit(solution)/shard_map/reduce_sum | solution.py:114
  449.2 11.8 %fusion.10 = f32[128,128,256]{2,1,0:T(8,128)} fusion(bf16[128,128,256]{2,1,0:T(8,128)(2,1)} %all-to-all-done.1, f32[128,128,128]{2,1,0:T(8,128)} %copy-done.2, f32[128,128]{1,0:T(8,128)S(1)} %gather_fusion.8, f32[128,128]{1,0:T(8,128)S(1)} %bitcast.45, pred[128]{0:T(512)(128)(4,1)S(1)} %compare_reduce_fusion), kind=kOutput, calls=%fused_computation.36 | convolution fusion | flops 1084227584 | bytes 33685632 | tf_op jit(solution)/shard_map/gij,gid->gjd/dot_general | solution.py:105
  461.0 20.6 %multiply_subtract_fusion = f32[12,128,256]{2,0,1:T(8,128)S(1)} fusion(f32[128,128,256]{2,1,0:T(8,128)} %fusion.10, bf16[12,128,256]{2,1,0:T(8,128)(2,1)S(1)} %constant_dynamic-slice_fusion, f32[12,128]{0,1:T(8,128)S(1)} %fusion.27, s32[128]{0:T(128)S(1)} %get-tuple-element.3), kind=kOutput, calls=%fused_computation.42 | convolution fusion | flops 605160960 | bytes 19143168 | tf_op jit(solution)/shard_map/sb,sjd->bjd/dot_general | solution.py:112
  481.6 2.1 copy.47
  483.7 2.8 all-gather
  486.5 0.6 reshape.327
  487.1 8.5 %all-gather.3.cloned.1.call-done = f32[24,128,256]{2,1,0:T(8,128)} async-done(((f32[12,128,256]{2,1,0:T(8,128)}), f32[24,128,256]{2,1,0:T(8,128)}) %all-gather.3.cloned.1.call-update) | async-done | bytes 3145744 | tf_op jit(solution)/shard_map/all_gather | solution.py:118
  495.6 3.8 copy.58
  (50 shorter events, 4.5 us)
Async XLA Ops:
  7.2 18.7 %copy-start = (bf16[3072,256]{1,0:T(8,128)(2,1)S(1)}, bf16[3072,256]{1,0:T(8,128)(2,1)}, u32[]{:S(2)}) copy-start(bf16[3072,256]{1,0:T(8,128)(2,1)} %param.5) | copy-start | bytes 4718596
  9.5 30.0 %all-to-all-start = ((s32[128,1,1]{2,1,0:T(1,128)}), s32[128,1,1]{2,1,0:T(1,128)S(1)}, u32[]{:S(2)}, u32[]{:S(2)}) async-start(s32[128,1,1]{2,1,0:T(1,128)} %copy.38), calls=%async_computation | async-start | bytes 131072 | tf_op jit(solution)/shard_map/all_to_all | solution.py:46
  39.5 14.2 %copy-start.5 = (bf16[3072,256]{1,0:T(8,128)(2,1)S(1)}, bf16[3072,256]{1,0:T(8,128)(2,1)}, u32[]{:S(2)}) copy-start(bf16[3072,256]{1,0:T(8,128)(2,1)} %param.6) | copy-start | bytes 4718596
  39.5 196.1 %all-to-all-start.1 = ((bf16[128,128,256]{2,1,0:T(8,128)(2,1)}), bf16[128,128,256]{2,1,0:T(8,128)(2,1)}, u32[]{:S(2)}, u32[]{:S(2)}) async-start(bf16[128,128,256]{2,1,0:T(8,128)(2,1)} %broadcast_select_fusion), calls=%async_computation.1 | async-start | bytes 16777216 | tf_op jit(solution)/shard_map/all_to_all | solution.py:46
  250.8 3.2 copy-start.2
  259.4 21.3 %all-to-all-start.2 = ((f32[128,1,128]{2,1,0:T(1,128)}), f32[128,1,128]{2,1,0:T(1,128)S(1)}, u32[]{:S(2)}, u32[]{:S(2)}) async-start(f32[128,1,128]{2,1,0:T(1,128)} %bitcast.5), calls=%async_computation.2 | async-start | bytes 131072 | tf_op jit(solution)/shard_map/all_to_all | solution.py:46
  281.9 4.3 collective-permute-start.1
  285.4 1.2 collective-permute-start
  287.9 17.0 %all-to-all-start.3 = ((f32[128,1,128]{2,1,0:T(1,128)}), f32[128,1,128]{2,1,0:T(1,128)S(1)}, u32[]{:S(2)}, u32[]{:S(2)}) async-start(f32[128,1,128]{2,1,0:T(1,128)} %bitcast.8), calls=%async_computation.3 | async-start | bytes 131072 | tf_op jit(solution)/shard_map/all_to_all | solution.py:46
  304.9 5.9 %copy-start.3 = (f32[128,128,128]{2,1,0:T(8,128)S(1)}, f32[128,128,128]{2,1,0:T(8,128)}, u32[]{:S(2)}) copy-start(f32[128,128,128]{2,1,0:T(8,128)} %copy-done.2) | copy-start | bytes 25165828
  346.8 3.4 collective-permute-start.3
  349.4 1.2 collective-permute-start.2
  409.4 3.5 collective-permute-start.5
  412.1 1.2 collective-permute-start.4
  413.3 28.6 %copy-start.4 = (f32[24,128]{1,0:T(8,128)}, f32[24,128]{1,0:T(8,128)S(1)}, u32[]{:S(2)}) copy-start(f32[24,128]{1,0:T(8,128)S(1)} %add_multiply_fusion) | copy-start | bytes 36868
  414.7 16.7 %all-to-all-start.7 = ((f32[128,1,128]{2,1,0:T(1,128)}), f32[128,1,128]{2,1,0:T(1,128)S(1)}, u32[]{:S(2)}, u32[]{:S(2)}) async-start(f32[128,1,128]{2,1,0:T(1,128)} %bitcast.19), calls=%async_computation.7 | async-start | bytes 131072 | tf_op jit(solution)/shard_map/all_to_all | solution.py:46
  420.8 74.8 %all-gather.3.cloned.1.call-start = ((), (), s32[]{:S(2)}) async-start(), calls=%async_computation.8 | async-start | bytes 4718592 | tf_op jit(solution)/shard_map/all_gather | solution.py:118
  461.0 38.4 %copy-start.1 = (bf16[3072,256]{1,0:T(8,128)(2,1)S(1)}, bf16[3072,256]{1,0:T(8,128)(2,1)}, u32[]{:S(2)}) copy-start(bf16[3072,256]{1,0:T(8,128)(2,1)} %param.5) | copy-start | bytes 4718596
Sparse Core Ops, SparseCore 0:
  483.8 11.7 all-gather.2

commit v2 on v1

--- a/solution.py
+++ b/solution.py
@@ -1,6 +1,10 @@
+import functools
+
 import jax
 import jax.numpy as jnp
 from jax import lax
+from jax.experimental import pallas as pl
+from jax.experimental.pallas import tpu as pltpu
 from jax.sharding import PartitionSpec as P
 
 BLOCK = 128
@@ -9,6 +13,97 @@
 
 EPSILON = 0.05
 NEG_BIG = -1e30
+INV_EPS = 1.0 / EPSILON
+PAIRS_STEP = 16
+
+
+def as_column(row):
+    side = row.shape[1]
+    return jnp.transpose(jnp.broadcast_to(row, (side, side)))
+
+
+def sweep_kernel(grid_ref, dual_ref, out_ref):
+    def one(p, carry):
+        dual_col = as_column(dual_ref[pl.ds(p, 1), :])
+        scores = (dual_col - grid_ref[p]) * INV_EPS
+        peak = jnp.max(scores, axis=0, keepdims=True)
+        mass = jnp.sum(jnp.exp(scores - peak), axis=0, keepdims=True)
+        out_ref[pl.ds(p, 1), :] = peak + jnp.log(mass)
+        return carry
+
+    lax.fori_loop(0, grid_ref.shape[0], one, 0)
+
+
+def sweep(grids, duals):
+    pairs, side, _ = grids.shape
+    return pl.pallas_call(
+        sweep_kernel,
+        grid=(pairs // PAIRS_STEP,),
+        in_specs=[
+            pl.BlockSpec((PAIRS_STEP, side, side), lambda s: (s, 0, 0)),
+            pl.BlockSpec((PAIRS_STEP, side), lambda s: (s, 0)),
+        ],
+        out_specs=pl.BlockSpec((PAIRS_STEP, side), lambda s: (s, 0)),
+        out_shape=jax.ShapeDtypeStruct((pairs, side), jnp.float32),
+        cost_estimate=pl.CostEstimate(
+            flops=8 * pairs * side * side,
+            transcendentals=pairs * side * side,
+            bytes_accessed=4 * pairs * side * (side + 2),
+        ),
+    )(grids, duals)
+
+
+def gradient_kernel(keys_ref, grid_t_ref, source_ref, target_ref, rows_ref, half_ref, out_ref):
+    step = pl.program_id(0)
+
+    @pl.when(step == 0)
+    def _():
+        out_ref[...] = jnp.zeros_like(out_ref)
+
+    def one(p, carry):
+        key = keys_ref[step * PAIRS_STEP + p]
+
+        @pl.when(key >= 0)
+        def _():
+            target_col = as_column(target_ref[pl.ds(p, 1), :])
+            plan_t = jnp.exp((source_ref[pl.ds(p, 1), :] + target_col - grid_t_ref[p]) * INV_EPS)
+            mass = jnp.sum(plan_t, axis=1, keepdims=True)
+            numerator = jnp.dot(
+                plan_t.astype(jnp.bfloat16), rows_ref[p], preferred_element_type=jnp.float32
+            )
+            out_ref[key] += half_ref[key].astype(jnp.float32) * mass - numerator
+
+        return carry
+
+    lax.fori_loop(0, PAIRS_STEP, one, 0)
+
+
+def gradient_sums(keys, grids_t, source_duals, target_duals, rows, half_targets):
+    pairs, side, _ = grids_t.shape
+    width = rows.shape[2]
+    half = half_targets.shape[0]
+    return pl.pallas_call(
+        gradient_kernel,
+        grid_spec=pltpu.PrefetchScalarGridSpec(
+            num_scalar_prefetch=1,
+            grid=(pairs // PAIRS_STEP,),
+            in_specs=[
+                pl.BlockSpec((PAIRS_STEP, side, side), lambda s, k: (s, 0, 0)),
+                pl.BlockSpec((PAIRS_STEP, side), lambda s, k: (s, 0)),
+                pl.BlockSpec((PAIRS_STEP, side), lambda s, k: (s, 0)),
+                pl.BlockSpec((PAIRS_STEP, side, width), lambda s, k: (s, 0, 0)),
+                pl.BlockSpec((half, side, width), lambda s, k: (0, 0, 0)),
+            ],
+            out_specs=pl.BlockSpec((half, side, width), lambda s, k: (0, 0, 0)),
+        ),
+        out_shape=jax.ShapeDtypeStruct((half, side, width), jnp.float32),
+        compiler_params=pltpu.CompilerParams(dimension_semantics=("arbitrary",)),
+        cost_estimate=pl.CostEstimate(
+            flops=2 * pairs * side * side * width + 8 * pairs * side * side,
+            transcendentals=pairs * side * side,
+            bytes_accessed=pairs * side * (4 * side + 2 * width) + half * side * width * 6,
+        ),
+    )(keys, grids_t, source_duals, target_duals, rows, half_targets)
 
 
 def squares(blocks_in):
@@ -19,9 +114,15 @@
     inner_dot = jnp.einsum(
         "gid,gjd->gij", source_rows, target_rows, preferred_element_type=jnp.float32
     )
+    inner_dot_t = jnp.einsum(
+        "gjd,gid->gji", target_rows, source_rows, preferred_element_type=jnp.float32
+    )
     source_sq = squares(source_rows)
     target_sq = squares(target_rows)
-    return (source_sq[:, :, None] + target_sq[:, None, :] - 2.0 * inner_dot) / source_rows.shape[2]
+    width = source_rows.shape[2]
+    grid = (source_sq[:, :, None] + target_sq[:, None, :] - 2.0 * inner_dot) / width
+    grid_t = (source_sq[:, None, :] + target_sq[:, :, None] - 2.0 * inner_dot_t) / width
+    return grid, grid_t
 
 
 def pair_lse(scores, axis):
@@ -68,9 +169,7 @@
     source_of_owner = jnp.max(jnp.where(matched, source_local[:, None], -1), axis=0)
     served = source_of_owner >= 0
     source_index = jnp.maximum(source_of_owner, 0)
-    outgoing = jnp.where(
-        served[:, None, None], own_sources[source_index], jnp.zeros((), src_points.dtype)
-    )
+    outgoing = own_sources[source_index]
     asked_ids = a2a(wanted)
     received = a2a(outgoing)
 
@@ -79,12 +178,12 @@
     half_pick = jnp.clip(half_key, 0, half_blocks - 1)
     own_half = lax.dynamic_slice_in_dim(own_targets, lower_block, half_blocks, 0)
     pair_targets = own_half[half_pick]
-    cost_grid = pair_costs(received, pair_targets)
+    cost_grid, cost_grid_t = pair_costs(received, pair_targets)
 
     target_half = jnp.zeros((half_blocks, block_len), jnp.float32)
     for round_no in range(ITERS):
         target_here = target_half[half_pick]
-        row_lse = pair_lse((target_here[:, None, :] - cost_grid) / EPSILON, 2)
+        row_lse = sweep(cost_grid_t, target_here)
         row_back = a2a(row_lse)
         maxima, totals = combine_by(row_back, source_of_owner, blocks)
         other_maxima, other_totals = swap_rep((maxima, totals))
@@ -95,25 +194,14 @@
         source_dual = -EPSILON * (merged + jnp.log(merged_totals))
         sent_duals = jnp.where(served[:, None], source_dual[source_index], 0.0)
         source_here = a2a(sent_duals)
-        column_lse = pair_lse((source_here[:, :, None] - cost_grid) / EPSILON, 1)
+        column_lse = sweep(cost_grid, source_here)
         col_max, col_tot = combine_by(column_lse, half_key, half_blocks)
         target_half = -EPSILON * (col_max + jnp.log(col_tot))
 
     target_here = target_half[half_pick]
-    plan = jnp.exp((source_here[:, :, None] + target_here[:, None, :] - cost_grid) / EPSILON)
-    plan = jnp.where(valid[:, None, None], plan, 0.0)
-    partial_value = jnp.einsum(
-        "gij,gid->gjd",
-        plan.astype(jnp.bfloat16),
-        received,
-        preferred_element_type=jnp.float32,
-    )
-    member = (half_key[:, None] == jnp.arange(half_blocks)[None, :]).astype(jnp.float32)
-    numerator = jnp.einsum("sb,sjd->bjd", member, partial_value, precision=lax.Precision.HIGHEST)
-    column_mass = jnp.einsum(
-        "sb,sj->bj", member, jnp.sum(plan, axis=1), precision=lax.Precision.HIGHEST
-    )
-    gradient_half = own_half.astype(jnp.float32) * column_mass[:, :, None] - numerator
+    gradient_half = gradient_sums(
+        half_key, cost_grid_t, source_here, target_here, received, own_half
+    )
     target_dual = lax.all_gather(target_half, "rep", axis=0, tiled=True)
     gradient = lax.all_gather(gradient_half, "rep", axis=0, tiled=True)
     return (

time: 512 us -> 573 us (1.12)
  Pallas kernels: 0 us -> 144 us
  other arithmetic: 101 us -> 27.9 us
  blocking collectives: 51.5 us -> 75.7 us
  matrix products: 42.1 us -> 18.7 us
  starting transfers between devices: 63.3 us -> 51.9 us
    pallas_call x0 -> x7, Pallas kernels: none -> 144 us  [the longest x6 127 us: sweep(): pl.pallas_call(sweep_kernel, grid=(pairs // PAIRS_STEP,), in_specs=[pl.Bl...]
    reduce_sum x7 -> x0, other arithmetic: 39.8 us -> none  [the longest x6 34 us: pair_lse(): masses = jnp.sum(jnp.exp(scores - jnp.expand_dims(peaks, axis)), axis=axis)]
    reduce_max x5 -> x0, other arithmetic: 27.5 us -> none  [pair_lse(): peaks = jnp.max(scores, axis=axis)]
    all_to_all x3 -> x4, blocking collectives: 48.7 us -> 73.9 us  [a2a(): return lax.all_to_all(value, 'pts', split_axis=0, concat_axis=0, tiled=True)]
    dot_general x3 -> x1, matrix products: 32.6 us -> 9.33 us  [pair_costs(): jnp.einsum('gjd,gid->gji', target_rows, source_rows, preferred_element_ty...]
    all_gather x1, waiting for transfers between devices: 8.54 us -> 25.6 us  [on_device(): gradient = lax.all_gather(gradient_half, 'rep', axis=0, tiled=True)]
    all_to_all x5 -> x4, waiting for transfers between devices: 193 us -> 178 us  [a2a(): return lax.all_to_all(value, 'pts', split_axis=0, concat_axis=0, tiled=True)]
    all_to_all x5 -> x4, starting transfers between devices: 53.7 us -> 43.6 us  [a2a(): return lax.all_to_all(value, 'pts', split_axis=0, concat_axis=0, tiled=True)]
  transfers between devices with their start and end apart: 12 -> 11, of which waited for: 11 -> 10; matrix products, arithmetic and copies ran while one was open for 7% -> 6% of each run, Pallas kernels for 0% -> 0%
where the time goes in v2:
time: 573 us; the launch traced here: 567 us
  waiting for transfers between devices  207 us (36%)
  Pallas kernels  144 us (25%)
  blocking collectives  75.7 us (13%)
  starting transfers between devices  51.9 us (9%)
  other arithmetic  27.9 us (5%)
  local copies, waits for them, and re-layouts  26.6 us (5%)
  matrix products  18.7 us (3%)
  between operations  15.5 us (3%)
    all_to_all x4, waiting for transfers between devices, a2a(): return lax.all_to_all(value, 'pts', split_axis=0, concat_axis=0, tiled=True)  178 us
    pallas_call x6, Pallas kernels, sweep(): pl.pallas_call(sweep_kernel, grid=(pairs // PAIRS_STEP,), in_specs=[pl.Bl...  127 us
    all_to_all x4, blocking collectives, a2a(): return lax.all_to_all(value, 'pts', split_axis=0, concat_axis=0, tiled=True)  73.9 us
    all_to_all x4, starting transfers between devices, a2a(): return lax.all_to_all(value, 'pts', split_axis=0, concat_axis=0, tiled=True)  43.6 us
    all_gather x1, waiting for transfers between devices, on_device(): gradient = lax.all_gather(gradient_half, 'rep', axis=0, tiled=True)  25.6 us
    pallas_call x1, Pallas kernels, gradient_sums(): pl.pallas_call(gradient_kernel, grid_spec=pltpu.PrefetchScalarGridSpec(nu...  17.5 us
  transfers between devices with their start and end apart: 11, of which 10 were waited for; matrix products, arithmetic and copies ran while one was open for 6% of the time, Pallas kernels for 0%

profile of v2, /device:TPU:1, one launch (start us, length us, event | category | flops | bytes accessed | tf_op | source)
XLA Modules:
  0.0 567.4 jit_solution(10397003076392509229)
XLA Ops:
  8.0 0.7 fusion.8
  8.6 0.1 select_reduce_fusion.13
  8.8 0.7 copy.22
  9.5 16.3 %all-to-all-start.1 = ((s32[128,1,1]{2,1,0:T(1,128)}), s32[128,1,1]{2,1,0:T(1,128)S(1)}, u32[]{:S(2)}, u32[]{:S(2)}) async-start(s32[128,1,1]{2,1,0:T(1,128)} %copy.22), calls=%async_computation.1 | async-start | bytes 131072 | tf_op jit(solution)/shard_map/all_to_all | solution.py:147
  25.9 6.4 %gather_fusion = bf16[128,128,256]{2,1,0:T(8,128)(2,1)} fusion(bf16[24,128,256]{2,1,0:T(8,128)(2,1)S(1)} %bitcast.41, s32[1024]{0:T(1024)S(1)} %pad_clamp_fusion.1), kind=kCustom, calls=%fused_computation | custom fusion | bytes 16777728 | tf_op jit(solution)/shard_map/gather | solution.py:172
  32.3 4.1 all-to-all-done.1
  36.4 9.9 %all-to-all-start = ((bf16[128,128,256]{2,1,0:T(8,128)(2,1)}), bf16[128,128,256]{2,1,0:T(8,128)(2,1)}, u32[]{:S(2)}, u32[]{:S(2)}) async-start(bf16[128,128,256]{2,1,0:T(8,128)(2,1)} %gather_fusion), calls=%async_computation | async-start | bytes 16777216 | tf_op jit(solution)/shard_map/all_to_all | solution.py:147
  46.3 1.2 constant_dynamic-slice_fusion.half_ref
  47.5 4.6 fusion.11
  52.2 6.4 %gather_fusion.1 = bf16[128,128,256]{2,1,0:T(8,128)(2,1)} fusion(bf16[12,128,256]{2,1,0:T(8,128)(2,1)S(1)} %constant_dynamic-slice_fusion.half_ref, s32[1024]{0:T(1024)S(1)} %pad_clamp_fusion), kind=kCustom, calls=%fused_computation.1 | custom fusion | bytes 16777728 | tf_op jit(solution)/shard_map/gather | solution.py:180
  58.7 1.2 gather_fusion.2
  59.9 5.6 multiply_reduce_fusion
  65.5 162.4 %all-to-all-done.rows_ref = bf16[128,128,256]{2,1,0:T(8,128)(2,1)} async-done(((bf16[128,128,256]{2,1,0:T(8,128)(2,1)}), bf16[128,128,256]{2,1,0:T(8,128)(2,1)}, u32[]{:S(2)}, u32[]{:S(2)}) %all-to-all-start) | async-done | bytes 8388640 | tf_op jit(solution)/shard_map/all_to_all | solution.py:147
  227.9 5.6 multiply_reduce_fusion.1
  233.5 9.3 %subtract_multiply_fusion.1.grid_ref.grid_t_ref = f32[128,128,128]{2,1,0:T(8,128)} fusion(f32[128,128]{1,0:T(8,128)S(1)} %multiply_reduce_fusion, f32[128,128]{1,0:T(8,128)S(1)} %multiply_reduce_fusion.1, bf16[128,128,256]{2,1,0:T(8,128)(2,1)} %gather_fusion.1, bf16[128,128,256]{2,1,0:T(8,128)(2,1)} %all-to-all-done.rows_ref), kind=kOutput, calls=%fused_computation.12 | convolution fusion | flops 1082130432 | bytes 25296896 | tf_op jit(solution)/shard_map/gjd,gid->gji/dot_general | solution.py:117
  242.8 21.1 %shard_map.76 = f32[128,128]{1,0:T(8,128)} custom-call(f32[128,128,128]{2,1,0:T(8,128)} %subtract_multiply_fusion.1.grid_ref.grid_t_ref, f32[128,128]{1,0:T(8,128)} %gather_fusion.2), custom_call_target="tpu_custom_call" | custom-call | flops 16777216 | bytes 8519680 | tf_op jit(solution)/shard_map/pallas_call | solution.py:39
  263.9 11.3 %all-to-all-start.2 = ((f32[128,1,128]{2,1,0:T(1,128)}), f32[128,1,128]{2,1,0:T(1,128)S(1)}, u32[]{:S(2)}, u32[]{:S(2)}) async-start(f32[128,1,128]{2,1,0:T(1,128)} %bitcast.49), calls=%async_computation.2 | async-start | bytes 131072 | tf_op jit(solution)/shard_map/all_to_all | solution.py:147
  275.2 10.6 %all-to-all-done.2 = f32[128,1,128]{2,1,0:T(1,128)S(1)} async-done(((f32[128,1,128]{2,1,0:T(1,128)}), f32[128,1,128]{2,1,0:T(1,128)S(1)}, u32[]{:S(2)}, u32[]{:S(2)}) %all-to-all-start.2) | async-done | bytes 65568 | tf_op jit(solution)/shard_map/all_to_all | solution.py:147
  285.8 0.6 select_reduce_fusion.5
  286.4 0.6 select_reduce_fusion.4
  287.0 3.5 collective-permute-start
  290.4 0.1 collective-permute-start.1
  290.6 1.1 collective-permute-done.1
  291.6 0.6 gather_fusion.3
  292.3 0.7 bitcast_select_fusion.2
  293.0 6.1 %all-to-all-start.3 = ((f32[128,1,128]{2,1,0:T(1,128)}), f32[128,1,128]{2,1,0:T(1,128)S(1)}, u32[]{:S(2)}, u32[]{:S(2)}) async-start(f32[128,1,128]{2,1,0:T(1,128)} %bitcast.9), calls=%async_computation.3 | async-start | bytes 131072 | tf_op jit(solution)/shard_map/all_to_all | solution.py:147
  299.2 9.3 %subtract_multiply_fusion.grid_ref = f32[128,128,128]{2,1,0:T(8,128)} fusion(f32[128,128]{1,0:T(8,128)S(1)} %multiply_reduce_fusion, f32[128,128]{1,0:T(8,128)S(1)} %multiply_reduce_fusion.1, bf16[128,128,256]{2,1,0:T(8,128)(2,1)} %all-to-all-done.rows_ref, bf16[128,128,256]{2,1,0:T(8,128)(2,1)} %gather_fusion.1), kind=kOutput, calls=%fused_computation.11 | convolution fusion | flops 1082130432 | bytes 25296896 | tf_op jit(solution)/shard_map/gid,gjd->gij/dot_general | solution.py:114
  308.5 1.1 all-to-all-done.3
  309.7 0.6 copy-done.3
  310.3 21.1 %shard_map.77 = f32[128,128]{1,0:T(8,128)} custom-call(f32[128,128,128]{2,1,0:T(8,128)} %subtract_multiply_fusion.grid_ref, f32[128,128]{1,0:T(8,128)} %bitcast.48), custom_call_target="tpu_custom_call" | custom-call | flops 16777216 | bytes 8519680 | tf_op jit(solution)/shard_map/pallas_call | solution.py:39
  331.4 1.1 select_reduce_fusion.11
  332.5 1.1 select_reduce_fusion.10
  333.7 1.2 gather_fusion.4
  334.9 21.1 %shard_map.78 = f32[128,128]{1,0:T(8,128)} custom-call(f32[128,128,128]{2,1,0:T(8,128)} %subtract_multiply_fusion.1.grid_ref.grid_t_ref, f32[128,128]{1,0:T(8,128)} %gather_fusion.4), custom_call_target="tpu_custom_call" | custom-call | flops 16777216 | bytes 8519680 | tf_op jit(solution)/shard_map/pallas_call | solution.py:39
  356.0 22.7 %all_to_all.65 = f32[128,1,128]{2,1,0:T(1,128)S(1)} all-to-all(f32[128,1,128]{2,1,0:T(1,128)} %bitcast.50), channel_id=1, replica_groups=mesh['pts'=128,'rep'=2] {'pts'}, dimensions={0} | all-to-all | bytes 131072 | tf_op jit(solution)/shard_map/all_to_all | solution.py:147
  378.7 0.6 select_reduce_fusion.3
  379.2 0.6 select_reduce_fusion.2
  379.8 2.0 collective-permute-start.3
  381.9 0.7 collective-permute-done.3
  382.6 0.3 collective-permute-done.2
  383.0 0.6 gather_fusion.5
  383.7 17.3 %all_to_all.66 = f32[128,1,128]{2,1,0:T(1,128)} all-to-all(f32[128,1,128]{2,1,0:T(1,128)S(1)} %bitcast.60), channel_id=1, replica_groups=mesh['pts'=128,'rep'=2] {'pts'}, dimensions={0} | all-to-all | bytes 131072 | tf_op jit(solution)/shard_map/all_to_all | solution.py:147
  401.0 21.1 %shard_map.79 = f32[128,128]{1,0:T(8,128)} custom-call(f32[128,128,128]{2,1,0:T(8,128)} %subtract_multiply_fusion.grid_ref, f32[128,128]{1,0:T(8,128)} %bitcast.51), custom_call_target="tpu_custom_call" | custom-call | flops 16777216 | bytes 8519680 | tf_op jit(solution)/shard_map/pallas_call | solution.py:39
  422.1 1.1 select_reduce_fusion.9
  423.3 1.1 select_reduce_fusion.8
  424.4 1.2 gather_fusion.6
  425.6 21.1 %shard_map.80 = f32[128,128]{1,0:T(8,128)} custom-call(f32[128,128,128]{2,1,0:T(8,128)} %subtract_multiply_fusion.1.grid_ref.grid_t_ref, f32[128,128]{1,0:T(8,128)} %gather_fusion.6), custom_call_target="tpu_custom_call" | custom-call | flops 16777216 | bytes 8519680 | tf_op jit(solution)/shard_map/pallas_call | solution.py:39
  446.7 16.9 %all_to_all.67 = f32[128,1,128]{2,1,0:T(1,128)S(1)} all-to-all(f32[128,1,128]{2,1,0:T(1,128)} %bitcast.52), channel_id=1, replica_groups=mesh['pts'=128,'rep'=2] {'pts'}, dimensions={0} | all-to-all | bytes 131072 | tf_op jit(solution)/shard_map/all_to_all | solution.py:147
  463.6 0.6 select_reduce_fusion.1
  464.2 0.6 select_reduce_fusion
  464.8 2.4 collective-permute-start.5
  467.3 0.7 collective-permute-done.5
  468.0 0.3 collective-permute-done.4
  468.4 0.6 gather_fusion.7
  469.1 17.0 %all_to_all.68 = f32[128,1,128]{2,1,0:T(1,128)} all-to-all(f32[128,1,128]{2,1,0:T(1,128)S(1)} %bitcast.59), channel_id=1, replica_groups=mesh['pts'=128,'rep'=2] {'pts'}, dimensions={0} | all-to-all | bytes 131072 | tf_op jit(solution)/shard_map/all_to_all | solution.py:147
  486.2 21.1 %shard_map.81 = f32[128,128]{1,0:T(8,128)} custom-call(f32[128,128,128]{2,1,0:T(8,128)} %subtract_multiply_fusion.grid_ref, f32[128,128]{1,0:T(8,128)} %bitcast.45), custom_call_target="tpu_custom_call" | custom-call | flops 16777216 | bytes 8519680 | tf_op jit(solution)/shard_map/pallas_call | solution.py:39
  507.3 1.1 select_reduce_fusion.7
  508.4 1.1 select_reduce_fusion.6
  509.6 1.2 gather_fusion.8
  510.8 17.5 %shard_map.82 = f32[12,128,256]{2,1,0:T(8,128)} custom-call(s32[128]{0:T(128)} %copy-done.4, f32[128,128,128]{2,1,0:T(8,128)} %subtract_multiply_fusion.1.grid_ref.grid_t_ref, f32[128,128]{1,0:T(8,128)} %bitcast.46, f32[128,128]{1,0:T(8,128)} %gather_fusion.8, bf16[128,128,256]{2,1,0:T(8,128)(2,1)} %all-to-all-done.rows_ref, bf16[12,128,256]{2,1,0:T(8,128)(2,1)} %copy-done.1), custom_call_target="tpu_custom_call" | custom-call | flops 1090519040 | bytes 19136512 | tf_op jit(solution)/shard_map/pallas_call | solution.py:85
  528.4 1.8 all-gather
  530.2 0.6 reshape.246
  530.8 25.6 %all-gather.3.cloned.1.call-done = f32[24,128,256]{2,1,0:T(8,128)} async-done(((f32[12,128,256]{2,1,0:T(8,128)}), f32[24,128,256]{2,1,0:T(8,128)}) %all-gather.3.cloned.1.call-update) | async-done | bytes 3145744 | tf_op jit(solution)/shard_map/all_gather | solution.py:206
  556.4 3.8 copy.31
  (31 shorter events, 0.7 us)
Async XLA Ops:
  7.2 18.7 %copy-start = (bf16[3072,256]{1,0:T(8,128)(2,1)S(1)}, bf16[3072,256]{1,0:T(8,128)(2,1)}, u32[]{:S(2)}) copy-start(bf16[3072,256]{1,0:T(8,128)(2,1)} %param.5) | copy-start | bytes 4718596
  9.5 26.9 %all-to-all-start.1 = ((s32[128,1,1]{2,1,0:T(1,128)}), s32[128,1,1]{2,1,0:T(1,128)S(1)}, u32[]{:S(2)}, u32[]{:S(2)}) async-start(s32[128,1,1]{2,1,0:T(1,128)} %copy.22), calls=%async_computation.1 | async-start | bytes 131072 | tf_op jit(solution)/shard_map/all_to_all | solution.py:147
  36.4 191.5 %all-to-all-start = ((bf16[128,128,256]{2,1,0:T(8,128)(2,1)}), bf16[128,128,256]{2,1,0:T(8,128)(2,1)}, u32[]{:S(2)}, u32[]{:S(2)}) async-start(bf16[128,128,256]{2,1,0:T(8,128)(2,1)} %gather_fusion), calls=%async_computation | async-start | bytes 16777216 | tf_op jit(solution)/shard_map/all_to_all | solution.py:147
  47.4 11.2 %copy-start.1 = (bf16[12,128,256]{2,1,0:T(8,128)(2,1)}, bf16[12,128,256]{2,1,0:T(8,128)(2,1)S(1)}, u32[]{:S(2)}) copy-start(bf16[12,128,256]{2,1,0:T(8,128)(2,1)S(1)} %constant_dynamic-slice_fusion.half_ref) | copy-start | bytes 2359300
  52.2 238.4 %copy-start.4 = (s32[128]{0:T(128)}, s32[128]{0:T(128)S(1)}, u32[]{:S(2)}) copy-start(s32[128]{0:T(128)S(1)} %get-tuple-element.3.keys_ref) | copy-start | bytes 1540
  263.9 21.9 %all-to-all-start.2 = ((f32[128,1,128]{2,1,0:T(1,128)}), f32[128,1,128]{2,1,0:T(1,128)S(1)}, u32[]{:S(2)}, u32[]{:S(2)}) async-start(f32[128,1,128]{2,1,0:T(1,128)} %bitcast.49), calls=%async_computation.2 | async-start | bytes 131072 | tf_op jit(solution)/shard_map/all_to_all | solution.py:147
  287.0 4.7 collective-permute-start
  290.4 1.2 collective-permute-start.1
  293.0 16.7 %all-to-all-start.3 = ((f32[128,1,128]{2,1,0:T(1,128)}), f32[128,1,128]{2,1,0:T(1,128)S(1)}, u32[]{:S(2)}, u32[]{:S(2)}) async-start(f32[128,1,128]{2,1,0:T(1,128)} %bitcast.9), calls=%async_computation.3 | async-start | bytes 131072 | tf_op jit(solution)/shard_map/all_to_all | solution.py:147
  299.2 257.2 %all-gather.3.cloned.1.call-start = ((), (), s32[]{:S(2)}) async-start(), calls=%async_computation.8 | async-start | bytes 4718592 | tf_op jit(solution)/shard_map/all_gather | solution.py:206
  309.7 0.6 copy-start.3
  379.8 2.8 collective-permute-start.3
  381.8 1.2 collective-permute-start.2
  464.8 3.3 collective-permute-start.5
  467.2 1.2 collective-permute-start.4
  468.4 59.9 %copy-start.2 = (f32[24,128]{1,0:T(8,128)}, f32[24,128]{1,0:T(8,128)S(1)}, u32[]{:S(2)}) copy-start(f32[24,128]{1,0:T(8,128)S(1)} %add_multiply_fusion) | copy-start | bytes 36868
Sparse Core Ops, SparseCore 0:
  528.5 27.8 all-gather.2

commit v3 on v2

--- a/solution.py
+++ b/solution.py
@@ -183,7 +183,7 @@
     target_half = jnp.zeros((half_blocks, block_len), jnp.float32)
     for round_no in range(ITERS):
         target_here = target_half[half_pick]
-        row_lse = sweep(cost_grid_t, target_here)
+        row_lse = pair_lse((target_here[:, None, :] - cost_grid) / EPSILON, 2)
         row_back = a2a(row_lse)
         maxima, totals = combine_by(row_back, source_of_owner, blocks)
         other_maxima, other_totals = swap_rep((maxima, totals))
@@ -194,7 +194,7 @@
         source_dual = -EPSILON * (merged + jnp.log(merged_totals))
         sent_duals = jnp.where(served[:, None], source_dual[source_index], 0.0)
         source_here = a2a(sent_duals)
-        column_lse = sweep(cost_grid, source_here)
+        column_lse = pair_lse((source_here[:, :, None] - cost_grid) / EPSILON, 1)
         col_max, col_tot = combine_by(column_lse, half_key, half_blocks)
         target_half = -EPSILON * (col_max + jnp.log(col_tot))
 

time: 573 us -> 501 us (0.87)
  Pallas kernels: 144 us -> 16.2 us
  other arithmetic: 27.9 us -> 86.1 us
  blocking collectives: 75.7 us -> 52.4 us
  waiting for transfers between devices: 207 us -> 219 us
  starting transfers between devices: 51.9 us -> 59.2 us
    pallas_call x6 -> x0, Pallas kernels: 127 us -> none  [sweep(): pl.pallas_call(sweep_kernel, grid=(pairs // PAIRS_STEP,), in_specs=[pl.Bl...]
    reduce_sum x0 -> x6, other arithmetic: none -> 34.2 us  [pair_lse(): masses = jnp.sum(jnp.exp(scores - jnp.expand_dims(peaks, axis)), axis=axis)]
    reduce_max x0 -> x5, other arithmetic: none -> 27.6 us  [pair_lse(): peaks = jnp.max(scores, axis=axis)]
    all_to_all x4 -> x3, blocking collectives: 73.9 us -> 48.6 us  [a2a(): return lax.all_to_all(value, 'pts', split_axis=0, concat_axis=0, tiled=True)]
    all_to_all x4 -> x5, waiting for transfers between devices: 178 us -> 189 us  [a2a(): return lax.all_to_all(value, 'pts', split_axis=0, concat_axis=0, tiled=True)]
    all_to_all x4 -> x5, starting transfers between devices: 43.6 us -> 50.1 us  [a2a(): return lax.all_to_all(value, 'pts', split_axis=0, concat_axis=0, tiled=True)]
  transfers between devices with their start and end apart: 11 -> 12, of which waited for: 10 -> 11; matrix products, arithmetic and copies ran while one was open for 6% -> 7% of each run, Pallas kernels for 0% -> 0%
where the time goes in v3:
time: 501 us; the launch traced here: 495 us
  waiting for transfers between devices  219 us (44%)
  other arithmetic  86.1 us (17%)
  starting transfers between devices  59.2 us (12%)
  blocking collectives  52.4 us (10%)
  local copies, waits for them, and re-layouts  27.4 us (5%)
  matrix products  18.8 us (4%)
  Pallas kernels  16.2 us (3%)
  between operations  15.5 us (3%)
    all_to_all x5, waiting for transfers between devices, a2a(): return lax.all_to_all(value, 'pts', split_axis=0, concat_axis=0, tiled=True)  189 us
    all_to_all x5, starting transfers between devices, a2a(): return lax.all_to_all(value, 'pts', split_axis=0, concat_axis=0, tiled=True)  50.1 us
    all_to_all x3, blocking collectives, a2a(): return lax.all_to_all(value, 'pts', split_axis=0, concat_axis=0, tiled=True)  48.6 us
    reduce_sum x6, other arithmetic, pair_lse(): masses = jnp.sum(jnp.exp(scores - jnp.expand_dims(peaks, axis)), axis=axis)  34.2 us
    reduce_max x5, other arithmetic, pair_lse(): peaks = jnp.max(scores, axis=axis)  27.6 us
    all_gather x1, waiting for transfers between devices, on_device(): gradient = lax.all_gather(gradient_half, 'rep', axis=0, tiled=True)  26.6 us
    pallas_call x1, Pallas kernels, gradient_sums(): pl.pallas_call(gradient_kernel, grid_spec=pltpu.PrefetchScalarGridSpec(nu...  16.2 us
    reduce_sum x2, other arithmetic, squares(): return jnp.sum(jnp.square(blocks_in.astype(jnp.float32)), axis=-1)  11.2 us
  transfers between devices with their start and end apart: 12, of which 11 were waited for; matrix products, arithmetic and copies ran while one was open for 7% of the time, Pallas kernels for 0%

profile of v3, /device:TPU:1, one launch (start us, length us, event | category | flops | bytes accessed | tf_op | source)
XLA Modules:
  0.0 494.7 jit_solution(3614946841371771481)
XLA Ops:
  8.0 0.7 fusion.14
  8.8 0.7 copy.16
  9.5 16.3 %all-to-all-start = ((s32[128,1,1]{2,1,0:T(1,128)}), s32[128,1,1]{2,1,0:T(1,128)S(1)}, u32[]{:S(2)}, u32[]{:S(2)}) async-start(s32[128,1,1]{2,1,0:T(1,128)} %copy.16), calls=%async_computation | async-start | bytes 131072 | tf_op jit(solution)/shard_map/all_to_all | solution.py:147
  25.9 6.3 %gather_fusion.1 = bf16[128,128,256]{2,1,0:T(8,128)(2,1)} fusion(bf16[24,128,256]{2,1,0:T(8,128)(2,1)S(1)} %bitcast.35, s32[1024]{0:T(1024)S(1)} %pad_clamp_fusion), kind=kCustom, calls=%fused_computation.1 | custom fusion | bytes 16777728 | tf_op jit(solution)/shard_map/gather | solution.py:172
  32.2 4.2 all-to-all-done
  36.4 9.9 %all-to-all-start.1 = ((bf16[128,128,256]{2,1,0:T(8,128)(2,1)}), bf16[128,128,256]{2,1,0:T(8,128)(2,1)}, u32[]{:S(2)}, u32[]{:S(2)}) async-start(bf16[128,128,256]{2,1,0:T(8,128)(2,1)} %gather_fusion.1), calls=%async_computation.1 | async-start | bytes 16777216 | tf_op jit(solution)/shard_map/all_to_all | solution.py:147
  46.3 1.2 constant_dynamic-slice_fusion.half_ref
  47.5 4.6 fusion.17
  52.2 6.4 %gather_fusion.2 = bf16[128,128,256]{2,1,0:T(8,128)(2,1)} fusion(bf16[12,128,256]{2,1,0:T(8,128)(2,1)S(1)} %constant_dynamic-slice_fusion.half_ref, s32[1024]{0:T(1024)S(1)} %pad_clamp_fusion.1), kind=kCustom, calls=%fused_computation.2 | custom fusion | bytes 16777728 | tf_op jit(solution)/shard_map/gather | solution.py:180
  58.6 0.6 gather_fusion
  59.3 5.6 %multiply_reduce_fusion = f32[128,128]{1,0:T(8,128)S(1)} fusion(bf16[128,128,256]{2,1,0:T(8,128)(2,1)} %gather_fusion.2), kind=kLoop, calls=%fused_computation.9 | loop fusion | flops 12566528 | bytes 8454144 | tf_op jit(solution)/shard_map/reduce_sum | solution.py:110
  64.9 163.1 %all-to-all-done.1.rows_ref = bf16[128,128,256]{2,1,0:T(8,128)(2,1)} async-done(((bf16[128,128,256]{2,1,0:T(8,128)(2,1)}), bf16[128,128,256]{2,1,0:T(8,128)(2,1)}, u32[]{:S(2)}, u32[]{:S(2)}) %all-to-all-start.1) | async-done | bytes 8388640 | tf_op jit(solution)/shard_map/all_to_all | solution.py:147
  228.0 5.6 %multiply_reduce_fusion.1 = f32[128,128]{1,0:T(8,128)S(1)} fusion(bf16[128,128,256]{2,1,0:T(8,128)(2,1)} %all-to-all-done.1.rows_ref), kind=kLoop, calls=%fused_computation.10 | loop fusion | flops 12566528 | bytes 8454144 | tf_op jit(solution)/shard_map/reduce_sum | solution.py:110
  233.6 9.2 %fusion = (f32[128,128]{1,0:T(8,128)S(1)}, f32[128,128,128]{2,1,0:T(8,128)S(1)}) fusion(f32[128,128]{1,0:T(8,128)S(1)} %gather_fusion, bf16[128,128,256]{2,1,0:T(8,128)(2,1)} %all-to-all-done.1.rows_ref, bf16[128,128,256]{2,1,0:T(8,128)(2,1)} %gather_fusion.2, f32[128,128]{1,0:T(8,128)S(1)} %multiply_reduce_fusion, f32[128,128]{1,0:T(8,128)S(1)} %multiply_reduce_fusion.1), kind=kOutput, calls=%fused_computation.25 | convolution fusion | flops 1088405504 | bytes 25427968 | tf_op jit(solution)/shard_map/gid,gjd->gij/dot_general | solution.py:114
  242.9 3.2 copy-done.1
  246.1 4.7 exponential_reduce_fusion.5
  250.8 0.6 log_add_fusion.5
  251.5 11.1 %all-to-all-start.2 = ((f32[128,1,128]{2,1,0:T(1,128)}), f32[128,1,128]{2,1,0:T(1,128)S(1)}, u32[]{:S(2)}, u32[]{:S(2)}) async-start(f32[128,1,128]{2,1,0:T(1,128)} %bitcast.5), calls=%async_computation.2 | async-start | bytes 131072 | tf_op jit(solution)/shard_map/all_to_all | solution.py:147
  262.6 10.4 %all-to-all-done.2 = f32[128,1,128]{2,1,0:T(1,128)S(1)} async-done(((f32[128,1,128]{2,1,0:T(1,128)}), f32[128,1,128]{2,1,0:T(1,128)S(1)}, u32[]{:S(2)}, u32[]{:S(2)}) %all-to-all-start.2) | async-done | bytes 65568 | tf_op jit(solution)/shard_map/all_to_all | solution.py:147
  273.1 0.6 select_reduce_fusion.5
  273.6 0.6 select_reduce_fusion.4
  274.2 3.5 collective-permute-start
  277.8 1.1 collective-permute-done.1
  278.9 0.6 gather_fusion.3
  279.5 0.7 bitcast_select_fusion.2
  280.3 6.6 %all-to-all-start.3 = ((f32[128,1,128]{2,1,0:T(1,128)}), f32[128,1,128]{2,1,0:T(1,128)S(1)}, u32[]{:S(2)}, u32[]{:S(2)}) async-start(f32[128,1,128]{2,1,0:T(1,128)} %bitcast.8), calls=%async_computation.3 | async-start | bytes 131072 | tf_op jit(solution)/shard_map/all_to_all | solution.py:147
  286.9 10.7 %all-to-all-done.3 = f32[128,1,128]{2,1,0:T(1,128)S(1)} async-done(((f32[128,1,128]{2,1,0:T(1,128)}), f32[128,1,128]{2,1,0:T(1,128)S(1)}, u32[]{:S(2)}, u32[]{:S(2)}) %all-to-all-start.3) | async-done | bytes 65568 | tf_op jit(solution)/shard_map/all_to_all | solution.py:147
  297.6 5.8 %fusion.1 = f32[128,128]{1,0:T(8,128)S(1)} fusion(f32[128,128,128]{2,1,0:T(8,128)} %copy-done.1, f32[128,128]{1,0:T(8,128)S(1)} %bitcast.42), kind=kLoop, calls=%fused_computation.26 | loop fusion | flops 6275072 | bytes 8519680 | tf_op jit(solution)/shard_map/reduce_max | solution.py:129
  303.5 4.9 exponential_reduce_fusion.4
  309.0 0.6 gather_fusion.4
  309.7 5.6 %fusion.2 = f32[128,128]{1,0:T(8,128)S(1)} fusion(f32[128,128,128]{2,1,0:T(8,128)} %copy-done.1, f32[128,128]{1,0:T(8,128)S(1)} %gather_fusion.4), kind=kLoop, calls=%fused_computation.27 | loop fusion | flops 6275072 | bytes 8519680 | tf_op jit(solution)/shard_map/reduce_max | solution.py:129
  315.3 6.9 %exponential_reduce_fusion.3 = f32[128,128]{1,0:T(8,128)S(1)} fusion(f32[128,128,128]{2,1,0:T(8,128)} %copy-done.1, f32[128,128]{1,0:T(8,128)S(1)} %fusion.2, f32[128,128]{1,0:T(8,128)S(1)} %gather_fusion.4), kind=kLoop, calls=%fused_computation.18 | loop fusion | flops 8372224 | bytes 8585216 | tf_op jit(solution)/shard_map/reduce_sum | solution.py:130
  322.3 16.1 %all_to_all.49 = f32[128,1,128]{2,1,0:T(1,128)S(1)} all-to-all(f32[128,1,128]{2,1,0:T(1,128)S(1)} %bitcast.47), channel_id=1, replica_groups=mesh['pts'=128,'rep'=2] {'pts'}, dimensions={0} | all-to-all | bytes 131072 | tf_op jit(solution)/shard_map/all_to_all | solution.py:147
  338.4 0.6 select_reduce_fusion.3
  338.9 0.6 select_reduce_fusion.2
  339.5 2.6 collective-permute-start.3
  342.2 0.7 collective-permute-done.3
  342.9 0.3 collective-permute-done.2
  343.3 0.6 gather_fusion.5
  344.0 16.4 %all_to_all.50 = f32[128,1,128]{2,1,0:T(1,128)S(1)} all-to-all(f32[128,1,128]{2,1,0:T(1,128)S(1)} %bitcast.55), channel_id=1, replica_groups=mesh['pts'=128,'rep'=2] {'pts'}, dimensions={0} | all-to-all | bytes 131072 | tf_op jit(solution)/shard_map/all_to_all | solution.py:147
  360.4 5.2 %fusion.3 = f32[128,128]{1,0:T(8,128)S(1)} fusion(f32[128,128,128]{2,1,0:T(8,128)} %copy-done.1, f32[128,128]{1,0:T(8,128)S(1)} %bitcast.44), kind=kLoop, calls=%fused_computation.28 | loop fusion | flops 6275072 | bytes 8519680 | tf_op jit(solution)/shard_map/reduce_max | solution.py:129
  365.7 5.4 %exponential_reduce_fusion.2 = f32[128,128]{1,0:T(8,128)S(1)} fusion(f32[128,128,128]{2,1,0:T(8,128)} %copy-done.1, f32[128,128]{1,0:T(8,128)S(1)} %fusion.3, f32[128,128]{1,0:T(8,128)S(1)} %bitcast.45), kind=kLoop, calls=%fused_computation.16 | loop fusion | flops 8372224 | bytes 8585216 | tf_op jit(solution)/shard_map/reduce_sum | solution.py:130
  371.7 0.6 gather_fusion.6
  372.4 5.6 %fusion.4 = f32[128,128]{1,0:T(8,128)S(1)} fusion(f32[128,128,128]{2,1,0:T(8,128)} %copy-done.1, f32[128,128]{1,0:T(8,128)S(1)} %gather_fusion.6), kind=kLoop, calls=%fused_computation.29 | loop fusion | flops 6275072 | bytes 8519680 | tf_op jit(solution)/shard_map/reduce_max | solution.py:129
  378.0 6.9 %exponential_reduce_fusion.1 = f32[128,128]{1,0:T(8,128)S(1)} fusion(f32[128,128,128]{2,1,0:T(8,128)} %copy-done.1, f32[128,128]{1,0:T(8,128)S(1)} %fusion.4, f32[128,128]{1,0:T(8,128)S(1)} %gather_fusion.6), kind=kLoop, calls=%fused_computation.14 | loop fusion | flops 8372224 | bytes 8585216 | tf_op jit(solution)/shard_map/reduce_sum | solution.py:130
  384.9 16.1 %all_to_all.51 = f32[128,1,128]{2,1,0:T(1,128)S(1)} all-to-all(f32[128,1,128]{2,1,0:T(1,128)S(1)} %bitcast.48), channel_id=1, replica_groups=mesh['pts'=128,'rep'=2] {'pts'}, dimensions={0} | all-to-all | bytes 131072 | tf_op jit(solution)/shard_map/all_to_all | solution.py:147
  401.1 0.6 select_reduce_fusion.1
  401.6 0.6 select_reduce_fusion
  402.2 2.7 collective-permute-start.5
  405.0 0.7 collective-permute-done.5
  405.7 0.3 collective-permute-done.4
  406.1 0.6 gather_fusion.7
  406.8 0.7 bitcast_select_fusion
  407.5 6.1 %all-to-all-start.7 = ((f32[128,1,128]{2,1,0:T(1,128)}), f32[128,1,128]{2,1,0:T(1,128)S(1)}, u32[]{:S(2)}, u32[]{:S(2)}) async-start(f32[128,1,128]{2,1,0:T(1,128)} %bitcast.19), calls=%async_computation.7 | async-start | bytes 131072 | tf_op jit(solution)/shard_map/all_to_all | solution.py:147
  413.7 9.6 %subtract_multiply_fusion.grid_t_ref = f32[128,128,128]{2,1,0:T(8,128)} fusion(f32[128,128]{1,0:T(8,128)S(1)} %multiply_reduce_fusion, f32[128,128]{1,0:T(8,128)S(1)} %multiply_reduce_fusion.1, bf16[128,128,256]{2,1,0:T(8,128)(2,1)} %gather_fusion.2, bf16[128,128,256]{2,1,0:T(8,128)(2,1)} %all-to-all-done.1.rows_ref), kind=kOutput, calls=%fused_computation.11 | convolution fusion | flops 1082130432 | bytes 25296896 | tf_op jit(solution)/shard_map/gjd,gid->gji/dot_general | solution.py:117
  423.2 0.9 all-to-all-done.7
  424.2 5.3 %fusion.5 = f32[128,128]{1,0:T(8,128)S(1)} fusion(f32[128,128,128]{2,1,0:T(8,128)} %copy-done.1, f32[128,128]{1,0:T(8,128)S(1)} %bitcast.39), kind=kLoop, calls=%fused_computation.30 | loop fusion | flops 6275072 | bytes 8519680 | tf_op jit(solution)/shard_map/reduce_max | solution.py:129
  429.4 5.4 %exponential_reduce_fusion = f32[128,128]{1,0:T(8,128)S(1)} fusion(f32[128,128,128]{2,1,0:T(8,128)} %copy-done.1, f32[128,128]{1,0:T(8,128)S(1)} %fusion.5, f32[128,128]{1,0:T(8,128)S(1)} %bitcast.40), kind=kLoop, calls=%fused_computation.12 | loop fusion | flops 8372224 | bytes 8585216 | tf_op jit(solution)/shard_map/reduce_sum | solution.py:130
  435.5 1.2 gather_fusion.8
  436.7 16.2 %shard_map.76 = f32[12,128,256]{2,1,0:T(8,128)} custom-call(s32[128]{0:T(128)} %copy-done.6, f32[128,128,128]{2,1,0:T(8,128)} %subtract_multiply_fusion.grid_t_ref, f32[128,128]{1,0:T(8,128)} %bitcast.41, f32[128,128]{1,0:T(8,128)} %gather_fusion.8, bf16[128,128,256]{2,1,0:T(8,128)(2,1)} %all-to-all-done.1.rows_ref, bf16[12,128,256]{2,1,0:T(8,128)(2,1)} %copy-done.3), custom_call_target="tpu_custom_call" | custom-call | flops 1090519040 | bytes 19136512 | tf_op jit(solution)/shard_map/pallas_call | solution.py:85
  452.9 3.7 all-gather
  456.7 0.6 reshape.324
  457.3 26.6 %all-gather.3.cloned.1.call-done = f32[24,128,256]{2,1,0:T(8,128)} async-done(((f32[12,128,256]{2,1,0:T(8,128)}), f32[24,128,256]{2,1,0:T(8,128)}) %all-gather.3.cloned.1.call-update) | async-done | bytes 3145744 | tf_op jit(solution)/shard_map/all_gather | solution.py:206
  483.8 3.8 copy.22
  (47 shorter events, 2.8 us)
Async XLA Ops:
  7.2 18.7 %copy-start = (bf16[3072,256]{1,0:T(8,128)(2,1)S(1)}, bf16[3072,256]{1,0:T(8,128)(2,1)}, u32[]{:S(2)}) copy-start(bf16[3072,256]{1,0:T(8,128)(2,1)} %param.5) | copy-start | bytes 4718596
  9.5 26.9 %all-to-all-start = ((s32[128,1,1]{2,1,0:T(1,128)}), s32[128,1,1]{2,1,0:T(1,128)S(1)}, u32[]{:S(2)}, u32[]{:S(2)}) async-start(s32[128,1,1]{2,1,0:T(1,128)} %copy.16), calls=%async_computation | async-start | bytes 131072 | tf_op jit(solution)/shard_map/all_to_all | solution.py:147
  36.4 191.6 %all-to-all-start.1 = ((bf16[128,128,256]{2,1,0:T(8,128)(2,1)}), bf16[128,128,256]{2,1,0:T(8,128)(2,1)}, u32[]{:S(2)}, u32[]{:S(2)}) async-start(bf16[128,128,256]{2,1,0:T(8,128)(2,1)} %gather_fusion.1), calls=%async_computation.1 | async-start | bytes 16777216 | tf_op jit(solution)/shard_map/all_to_all | solution.py:147
  47.5 11.1 %copy-start.3 = (bf16[12,128,256]{2,1,0:T(8,128)(2,1)}, bf16[12,128,256]{2,1,0:T(8,128)(2,1)S(1)}, u32[]{:S(2)}) copy-start(bf16[12,128,256]{2,1,0:T(8,128)(2,1)S(1)} %constant_dynamic-slice_fusion.half_ref) | copy-start | bytes 2359300
  52.2 234.7 %copy-start.6 = (s32[128]{0:T(128)}, s32[128]{0:T(128)S(1)}, u32[]{:S(2)}) copy-start(s32[128]{0:T(128)S(1)} %get-tuple-element.3.keys_ref) | copy-start | bytes 1540
  242.9 3.2 copy-start.1
  251.5 21.6 %all-to-all-start.2 = ((f32[128,1,128]{2,1,0:T(1,128)}), f32[128,1,128]{2,1,0:T(1,128)S(1)}, u32[]{:S(2)}, u32[]{:S(2)}) async-start(f32[128,1,128]{2,1,0:T(1,128)} %bitcast.5), calls=%async_computation.2 | async-start | bytes 131072 | tf_op jit(solution)/shard_map/all_to_all | solution.py:147
  274.2 4.7 collective-permute-start
  277.7 1.2 collective-permute-start.1
  280.3 17.3 %all-to-all-start.3 = ((f32[128,1,128]{2,1,0:T(1,128)}), f32[128,1,128]{2,1,0:T(1,128)S(1)}, u32[]{:S(2)}, u32[]{:S(2)}) async-start(f32[128,1,128]{2,1,0:T(1,128)} %bitcast.8), calls=%async_computation.3 | async-start | bytes 131072 | tf_op jit(solution)/shard_map/all_to_all | solution.py:147
  297.6 5.9 %copy-start.2 = (f32[128,128,128]{2,1,0:T(8,128)S(1)}, f32[128,128,128]{2,1,0:T(8,128)}, u32[]{:S(2)}) copy-start(f32[128,128,128]{2,1,0:T(8,128)} %copy-done.1) | copy-start | bytes 25165828
  339.5 3.4 collective-permute-start.3
  342.1 1.2 collective-permute-start.2
  402.2 3.5 collective-permute-start.5
  404.9 1.2 collective-permute-start.4
  406.1 17.1 %copy-start.4 = (f32[24,128]{1,0:T(8,128)}, f32[24,128]{1,0:T(8,128)S(1)}, u32[]{:S(2)}) copy-start(f32[24,128]{1,0:T(8,128)S(1)} %add_multiply_fusion) | copy-start | bytes 36868
  407.5 16.7 %all-to-all-start.7 = ((f32[128,1,128]{2,1,0:T(1,128)}), f32[128,1,128]{2,1,0:T(1,128)S(1)}, u32[]{:S(2)}, u32[]{:S(2)}) async-start(f32[128,1,128]{2,1,0:T(1,128)} %bitcast.19), calls=%async_computation.7 | async-start | bytes 131072 | tf_op jit(solution)/shard_map/all_to_all | solution.py:147
  413.6 70.2 %all-gather.3.cloned.1.call-start = ((), (), s32[]{:S(2)}) async-start(), calls=%async_computation.8 | async-start | bytes 4718592 | tf_op jit(solution)/shard_map/all_gather | solution.py:206
  424.2 10.6 %copy-start.5 = (f32[128,1,128]{2,1,0:T(1,128)}, f32[128,1,128]{2,1,0:T(1,128)S(1)}, u32[]{:S(2)}) copy-start(f32[128,1,128]{2,1,0:T(1,128)S(1)} %all-to-all-done.7) | copy-start | bytes 196612
Sparse Core Ops, SparseCore 0:
  453.1 30.7 all-gather.2
